TPU v7x, 32 devices: a whole 2x2x4 slice. The times are simulated.
32 devices in a mesh: group: 4 (over z), member: 8 (over y, x, core).
Axes of the slice: x: 2, y: 2, z: 4, core: 2. Of those that a mesh axis runs over, the one named last changes fastest.
Arguments:
- object_field: bfloat16 [2, 2, 2048, 4096], P(None, None, 'group', 'member'), may hold values from -4 to 4
- probe_modes: float32 [4, 2, 2, 128, 128], P('group'), may hold values from -7.2 to 7.2
- prop_phase: float32 [128, 128], replicated, may hold values from -3.140625 to 3.140625
- amplitude: float32 [4, 128, 128, 128], P('group', 'member'), may hold values from 0.5 to 4
- tile_owner: int32 [4, 128, 1], P('group', 'member'), may hold values from 0 to 7; in each aligned block of 16 rows (0 to 15, 16 to 31, ..., all dimensions but the last counted through in order) at most 4 rows name the same one
- corner: int32 [4, 128, 2], P('group', 'member'), may hold values from 0 to 384
Outputs:
- object_grad: float32 [2, 2, 2048, 4096], P(None, None, 'group', 'member')
- probe_grad: float32 [4, 2, 2, 128, 128], P('group')
Inputs may be any that keep to these rules, and one draw needn't show every extreme that they name: `tile_owner`: among the positions of one device at most 4 name the same tile column.
All inputs are finite; a program needn't handle non-finite values.
Results may differ from a plain program's by a relative error of at most 0.0003.
Values may be sent and summed in bfloat16 or wider, within the bound.
No kernel may reach another device: no remote copies, remote signals or barrier semaphores. Data moves between devices by JAX's collectives and lax.ppermute only.
A program may use at most 128 MiB of HBM per device.

v0:
```python
from functools import partial
import math

import jax
import jax.numpy as jnp
from jax import lax
from jax.experimental import pallas as pl
from jax.experimental.pallas import tpu as pltpu
from jax.sharding import PartitionSpec as P

DFT_PRECISION = lax.Precision.HIGH


def fourier_blocks(length, sign):
    counter = jnp.arange(length, dtype=jnp.int32)
    product = counter[:, None] * counter[None, :] % length
    angles = product.astype(jnp.float32) * (2.0 * math.pi / length)
    norming = 1.0 / math.sqrt(length)
    cosine = jnp.cos(angles) * norming
    sine_part = jnp.sin(angles) * (sign * norming)
    return jnp.stack([jnp.stack([cosine, sine_part]), jnp.stack([-sine_part, cosine])])


def transform(field, blocks):
    across = jnp.einsum("...chn,cdnk->...dhk", field, blocks, precision=DFT_PRECISION)
    return jnp.einsum("cdkn,...cnw->...dkw", blocks, across, precision=DFT_PRECISION)


def complex_times(left, right):
    left_re, left_im = (left[..., 0, :, :], left[..., 1, :, :])
    right_re, right_im = (right[..., 0, :, :], right[..., 1, :, :])
    return jnp.stack(
        [left_re * right_re - left_im * right_im, left_re * right_im + left_im * right_re], axis=-3
    )


def conj_times(left, right):
    left_re, left_im = (left[..., 0, :, :], left[..., 1, :, :])
    right_re, right_im = (right[..., 0, :, :], right[..., 1, :, :])
    return jnp.stack(
        [left_re * right_re + left_im * right_im, left_re * right_im - left_im * right_re], axis=-3
    )


def slot_numbers(targets, members, capacity):
    matches = (targets[:, None] == jnp.arange(members, dtype=jnp.int32)[None, :]).astype(jnp.int32)
    before = jnp.cumsum(matches, axis=0) - matches
    return targets * capacity + jnp.sum(before * matches, axis=1)


def selectors(offsets, patch_side, tile_cells, dtype):
    inner = jnp.arange(patch_side, dtype=jnp.int32)
    cells = jnp.arange(tile_cells, dtype=jnp.int32)
    hit = offsets[:, None, None] + inner[None, :, None] == cells[None, None, :]
    return hit.astype(dtype)


def cut_windows(tiles, requests, patch_side):
    tile_cells = tiles.shape[-1]
    valid = requests[:, 0].astype(jnp.bfloat16)
    row_sel = selectors(requests[:, 1], patch_side, tile_cells, jnp.bfloat16) * valid[:, None, None]
    col_sel = selectors(requests[:, 2], patch_side, tile_cells, jnp.bfloat16)
    rows = jnp.einsum("kit,sctu->kscui", row_sel, tiles, preferred_element_type=jnp.float32)
    rows = rows.astype(jnp.bfloat16)
    window = jnp.einsum("kscui,kju->kscij", rows, col_sel, preferred_element_type=jnp.float32)
    return window.astype(jnp.bfloat16)


def place_kernel(requests, peak, terms, out, total):
    slot = pl.program_id(0)
    slice_count = terms.shape[1]
    patch_side = terms.shape[-1]
    tile_cells = out.shape[-1]

    @pl.when(slot == 0)
    def _():
        total[...] = jnp.zeros_like(total)

    row = requests[slot, 1]
    col = requests[slot, 2]
    row_base = pl.multiple_of((row // 8) * 8, 8)
    col_base = pl.multiple_of((col // 128) * 128, 128)
    row_rest = row - row_base
    col_rest = col - col_base
    band_rows = patch_side + 8
    band_cols = 2 * patch_side
    row_pick = (
        lax.broadcasted_iota(jnp.int32, (band_rows, patch_side), 0)
        == lax.broadcasted_iota(jnp.int32, (band_rows, patch_side), 1) + row_rest
    ).astype(jnp.bfloat16)
    col_pick = (
        lax.broadcasted_iota(jnp.int32, (patch_side, band_cols), 1)
        == lax.broadcasted_iota(jnp.int32, (patch_side, band_cols), 0) + col_rest
    ).astype(jnp.bfloat16)
    pieces = []
    for layer in range(slice_count):
        for part in range(2):
            term = terms[0, layer, part]
            high = term.astype(jnp.bfloat16)
            low = (term - high.astype(jnp.float32)).astype(jnp.bfloat16)
            pieces += [high, low]
    side_by_side = jnp.concatenate(pieces, axis=1)
    shifted = jnp.dot(row_pick, side_by_side, preferred_element_type=jnp.float32)
    shifted = shifted.astype(jnp.bfloat16)
    stacked = jnp.concatenate(
        [shifted[:, index * patch_side:(index + 1) * patch_side] for index in range(len(pieces))],
        axis=0,
    )
    placed = jnp.dot(stacked, col_pick, preferred_element_type=jnp.float32)
    for layer in range(slice_count):
        for part in range(2):
            index = 2 * (2 * layer + part)
            band = (
                placed[index * band_rows:(index + 1) * band_rows]
                + placed[(index + 1) * band_rows:(index + 2) * band_rows]
            )
            window = total.at[layer, part, pl.ds(row_base, band_rows), pl.ds(col_base, band_cols)]
            window[...] = window[...] + band

    @pl.when(slot == pl.num_programs(0) - 1)
    def _():
        out[...] = total[:, :, :tile_cells, :tile_cells] / peak[0, 0]


def accumulate(terms, requests, peak, tile_cells):
    slot_count, slice_count = terms.shape[:2]
    patch_side = terms.shape[-1]
    grid_spec = pltpu.PrefetchScalarGridSpec(
        num_scalar_prefetch=1,
        grid=(slot_count,),
        in_specs=[
            pl.BlockSpec(memory_space=pltpu.SMEM),
            pl.BlockSpec(
                (1, slice_count, 2, patch_side, patch_side), lambda k, req: (k, 0, 0, 0, 0)
            ),
        ],
        out_specs=pl.BlockSpec(
            (slice_count, 2, tile_cells, tile_cells), lambda k, req: (0, 0, 0, 0)
        ),
        scratch_shapes=[
            pltpu.VMEM(
                (slice_count, 2, tile_cells + 8, tile_cells + patch_side), jnp.float32
            )
        ],
    )
    return pl.pallas_call(
        place_kernel,
        grid_spec=grid_spec,
        out_shape=jax.ShapeDtypeStruct((slice_count, 2, tile_cells, tile_cells), jnp.float32),
        compiler_params=pltpu.CompilerParams(dimension_semantics=("arbitrary",)),
    )(requests, peak.reshape(1, 1), terms)


def group_max(value):
    count = lax.axis_size("group")
    if count & (count - 1) == 0:
        step = 1
        while step < count:
            pairs = [(index, index ^ step) for index in range(count)]
            value = jnp.maximum(value, lax.ppermute(value, "group", pairs))
            step *= 2
        return value
    running = value
    pairs = [(index, (index + 1) % count) for index in range(count)]
    for _ in range(count - 1):
        value = lax.ppermute(value, "group", pairs)
        running = jnp.maximum(running, value)
    return running


def split_pair(value):
    high = value.astype(jnp.bfloat16)
    low = (value - high.astype(jnp.float32)).astype(jnp.bfloat16)
    return high, low


def times_right(value, pair):
    high, low = split_pair(value)
    return (
        jnp.dot(high, pair[0], preferred_element_type=jnp.float32)
        + jnp.dot(low, pair[0], preferred_element_type=jnp.float32)
        + jnp.dot(high, pair[1], preferred_element_type=jnp.float32)
    )


def times_left(pair, value):
    high, low = split_pair(value)
    return (
        jnp.dot(pair[0], high, preferred_element_type=jnp.float32)
        + jnp.dot(pair[0], low, preferred_element_type=jnp.float32)
        + jnp.dot(pair[1], high, preferred_element_type=jnp.float32)
    )


def fourier_2d(real, imag, across, down, inverse):
    side = real.shape[0]
    right = times_right(jnp.concatenate([real, imag], axis=0), across)
    real_c, real_s = right[:side, :side], right[:side, side:]
    imag_c, imag_s = right[side:, :side], right[side:, side:]
    if inverse:
        mid_real, mid_imag = real_c - imag_s, imag_c + real_s
    else:
        mid_real, mid_imag = real_c + imag_s, imag_c - real_s
    left = times_left(down, jnp.concatenate([mid_real, mid_imag], axis=1))
    c_real, c_imag = left[:side, :side], left[:side, side:]
    s_real, s_imag = left[side:, :side], left[side:, side:]
    if inverse:
        return c_real - s_imag, c_imag + s_real
    return c_real + s_imag, c_imag - s_real


def propagate_kernel(patch_ref, measured_ref, probe_ref, kern_ref, across_ref, down_ref,
                     grad_ref, probe_sum_ref):
    slot = pl.program_id(0)
    slice_count = patch_ref.shape[1]
    modes = probe_ref.shape[0]
    across = (across_ref[0], across_ref[1])
    down = (down_ref[0], down_ref[1])
    kern_real, kern_imag = kern_ref[0], kern_ref[1]
    waves = [(probe_ref[m, 0], probe_ref[m, 1]) for m in range(modes)]
    history = []
    leaving = None
    for layer in range(slice_count):
        history.append(waves)
        patch_real = patch_ref[0, layer, 0].astype(jnp.float32)
        patch_imag = patch_ref[0, layer, 1].astype(jnp.float32)
        leaving = [
            (wr * patch_real - wi * patch_imag, wr * patch_imag + wi * patch_real)
            for wr, wi in waves
        ]
        if layer < slice_count - 1:
            waves = []
            for lr, li in leaving:
                fr, fi = fourier_2d(lr, li, across, down, False)
                tr = kern_real * fr - kern_imag * fi
                ti = kern_real * fi + kern_imag * fr
                waves.append(fourier_2d(tr, ti, across, down, True))
    far = [fourier_2d(lr, li, across, down, False) for lr, li in leaving]
    intensity = None
    for fr, fi in far:
        power = fr * fr + fi * fi
        intensity = power if intensity is None else intensity + power
    factor = 1.0 - measured_ref[0] / jnp.sqrt(jnp.maximum(intensity, 1.0))
    back = [fourier_2d(fr * factor, fi * factor, across, down, True) for fr, fi in far]
    for layer in reversed(range(slice_count)):
        grad_real = None
        grad_imag = None
        for (wr, wi), (br, bi) in zip(history[layer], back):
            term_real = wr * br + wi * bi
            term_imag = wr * bi - wi * br
            grad_real = term_real if grad_real is None else grad_real + term_real
            grad_imag = term_imag if grad_imag is None else grad_imag + term_imag
        grad_ref[0, layer, 0] = grad_real
        grad_ref[0, layer, 1] = grad_imag
        patch_real = patch_ref[0, layer, 0].astype(jnp.float32)
        patch_imag = patch_ref[0, layer, 1].astype(jnp.float32)
        back = [
            (patch_real * br + patch_imag * bi, patch_real * bi - patch_imag * br)
            for br, bi in back
        ]
        if layer > 0:
            moved = []
            for br, bi in back:
                fr, fi = fourier_2d(br, bi, across, down, False)
                tr = kern_real * fr + kern_imag * fi
                ti = kern_real * fi - kern_imag * fr
                moved.append(fourier_2d(tr, ti, across, down, True))
            back = moved

    @pl.when(slot == 0)
    def _():
        probe_sum_ref[...] = jnp.zeros_like(probe_sum_ref)

    for mode, (br, bi) in enumerate(back):
        probe_sum_ref[mode, 0] = probe_sum_ref[mode, 0] + br
        probe_sum_ref[mode, 1] = probe_sum_ref[mode, 1] + bi


def dft_pairs(length):
    counter = jnp.arange(length, dtype=jnp.int32)
    product = counter[:, None] * counter[None, :] % length
    angles = product.astype(jnp.float32) * (2.0 * math.pi / length)
    norming = 1.0 / math.sqrt(length)
    cosine = jnp.cos(angles) * norming
    sine = jnp.sin(angles) * norming
    across = jnp.concatenate([cosine, sine], axis=1)
    down = jnp.concatenate([cosine, sine], axis=0)

    def pair(value):
        high = lax.reduce_precision(value, exponent_bits=8, mantissa_bits=7)
        return jnp.stack([high, value - high]).astype(jnp.bfloat16)

    return pair(across), pair(down)


def propagate(patches, measured, probe_modes, prop_phase):
    count, slice_count = patches.shape[:2]
    modes = probe_modes.shape[0]
    side = patches.shape[-1]
    kern = jnp.stack([jnp.cos(prop_phase), jnp.sin(prop_phase)])
    across, down = dft_pairs(side)
    whole = lambda shape: pl.BlockSpec(shape, lambda k: (0,) * len(shape))
    return pl.pallas_call(
        propagate_kernel,
        grid=(count,),
        in_specs=[
            pl.BlockSpec((1, slice_count, 2, side, side), lambda k: (k, 0, 0, 0, 0)),
            pl.BlockSpec((1, side, side), lambda k: (k, 0, 0)),
            whole((modes, 2, side, side)),
            whole((2, side, side)),
            whole((2, side, 2 * side)),
            whole((2, 2 * side, side)),
        ],
        out_specs=[
            pl.BlockSpec((1, slice_count, 2, side, side), lambda k: (k, 0, 0, 0, 0)),
            whole((modes, 2, side, side)),
        ],
        out_shape=[
            jax.ShapeDtypeStruct((count, slice_count, 2, side, side), jnp.float32),
            jax.ShapeDtypeStruct((modes, 2, side, side), jnp.float32),
        ],
        compiler_params=pltpu.CompilerParams(dimension_semantics=("arbitrary",)),
    )(patches, measured, probe_modes, kern, across, down)


def on_device(object_field, probe_modes, prop_phase, amplitude, tile_owner, corner):
    members = lax.axis_size("member")
    pos_dev = tile_owner.shape[1]
    capacity = max(2, (2 * pos_dev + members - 1) // members)
    slot_count = members * capacity
    tile_cells = object_field.shape[2]
    patch_side = prop_phase.shape[0]
    power = jnp.max(jnp.sum(probe_modes * probe_modes, axis=(1, 2)))
    peak_power = group_max(power) + 1e-06
    flat_slots = slot_numbers(tile_owner[0, :, 0], members, capacity)
    entries = jnp.concatenate([jnp.ones((pos_dev, 1), jnp.int32), corner[0]], axis=1)
    chosen = (flat_slots[:, None] == jnp.arange(slot_count, dtype=jnp.int32)[None, :]).astype(
        jnp.int32
    )
    outgoing = jnp.sum(chosen[:, :, None] * entries[:, None, :], axis=0)
    requests = lax.all_to_all(
        outgoing.reshape(members, capacity, 3), "member", split_axis=0, concat_axis=0, tiled=True
    ).reshape(slot_count, 3)
    sent = jnp.zeros((slot_count, patch_side, patch_side), jnp.float32).at[flat_slots].set(
        amplitude[0]
    )
    measured = lax.all_to_all(
        sent.reshape(members, capacity, patch_side, patch_side),
        "member",
        split_axis=0,
        concat_axis=0,
        tiled=True,
    ).reshape(slot_count, patch_side, patch_side)
    patches = cut_windows(object_field, requests, patch_side)
    gradients, adjoint_sum = propagate(patches, measured, probe_modes[0], prop_phase)
    probe_grad = lax.psum(adjoint_sum / pos_dev, "member")[None]
    object_grad = accumulate(gradients, requests, peak_power, tile_cells)
    return (object_grad, probe_grad)


def solution(mesh):
    return jax.shard_map(
        on_device,
        mesh=mesh,
        in_specs=(
            P(None, None, "group", "member"),
            P("group", None, None, None, None),
            P(),
            P("group", "member", None, None),
            P("group", "member", None),
            P("group", "member", None),
        ),
        out_specs=(P(None, None, "group", "member"), P("group", None, None, None, None)),
        check_vma=False,
    )
```

profile of v0, /device:TPU:0, one launch (start us, length us, event | category | flops | bytes accessed | tf_op | source)
XLA Modules:
  0.0 297.8 jit_solution(8880599816236795472)
XLA Ops:
  7.2 0.9 fusion.35
  8.1 0.9 select_reduce_fusion
  9.0 0.7 multiply_add_fusion
  9.7 0.7 concatenate.51
  11.2 5.2 %all-to-all-start = ((s32[8,4,3]{1,2,0:T(4,128)}), s32[8,4,3]{1,2,0:T(4,128)S(1)}, u32[]{:S(2)}, u32[]{:S(2)}) async-start(s32[8,4,3]{1,2,0:T(4,128)} %copy.16), calls=%async_computation | async-start | bytes 32768 | tf_op jit(solution)/shard_map/all_to_all | solution.py:341
  16.7 0.7 fusion.37
  17.4 1.1 cosine_bitcast_fusion
  18.4 0.7 pad_maximum_fusion.2.across_ref
  19.1 0.7 pad_maximum_fusion.4.down_ref
  20.4 1.6 broadcast_in_dim.4
  22.0 3.0 scatter_fusion
  25.0 4.4 %all-to-all-start.1 = ((f32[8,4,128,128]{3,2,1,0:T(8,128)}), f32[8,4,128,128]{3,2,1,0:T(8,128)}, u32[]{:S(2)}, u32[]{:S(2)}) async-start(f32[8,4,128,128]{3,2,1,0:T(8,128)} %bitcast.74), calls=%async_computation.1 | async-start | bytes 4194304 | tf_op jit(solution)/shard_map/all_to_all | solution.py:347
  29.6 2.6 fusion.52
  32.2 16.1 %fusion.14.patch_ref = bf16[32,2,2,128,128]{4,3,2,1,0:T(8,128)(2,1)} fusion(s32[32,128]{1,0:T(8,128)S(1)} %get-tuple-element.15, bf16[2,2,512,512]{3,2,1,0:T(8,128)(2,1)S(1)} %copy-done, bf16[32]{0:T(256)(128)(2,1)S(1)} %slice_bitcast_fusion.1, pred[32,128,512,1,1]{2,1,4,3,0:T(32,128)(4,1)} %fusion.52), kind=kOutput, calls=%fused_computation.12 | convolution fusion | flops 10752098304 | bytes 8405056 | tf_op jit(solution)/shard_map/kscui,kju->kscij/dot_general | solution.py:65
  48.3 7.7 %all-to-all-done.1 = f32[8,4,128,128]{3,2,1,0:T(8,128)} async-done(((f32[8,4,128,128]{3,2,1,0:T(8,128)}), f32[8,4,128,128]{3,2,1,0:T(8,128)}, u32[]{:S(2)}, u32[]{:S(2)}) %all-to-all-start.1) | async-done | bytes 2097184 | tf_op jit(solution)/shard_map/all_to_all | solution.py:347
  56.0 178.4 %shard_map.77 = (f32[32,2,2,128,128]{4,3,2,1,0:T(8,128)}, f32[2,2,128,128]{3,2,1,0:T(8,128)}) custom-call(bf16[32,2,2,128,128]{4,3,2,1,0:T(8,128)(2,1)} %fusion.14.patch_ref, f32[32,128,128]{2,1,0:T(8,128)} %bitcast.17.measured_ref, f32[2,2,128,128]{3,2,1,0:T(8,128)} %bitcast.76, f32[2,128,128]{2,1,0:T(8,128)} %pad_maximum_fusion.kern_ref, ...), custom_call_target="tpu_custom_call" | custom-call | tf_op jit(solution)/shard_map/pallas_call | solution.py:303
  234.4 1.7 multiply_bitcast_fusion
  236.8 1.6 collective-permute-start
  238.3 2.2 collective-permute-done
  241.8 4.0 %collective-permute-start.1 = (f32[]{:T(128)}, f32[]{:T(128)}, u32[]{:S(2)}, u32[]{:S(2)}) collective-permute-start(f32[]{:T(128)} %max.6), channel_id=1, source_target_pairs={{0,16},{8,24},{16,0},{24,8},{1,17},{9,25},{17,1},{25,9},{2,18},{10... | collective-permute-start | bytes 20 | tf_op jit(solution)/shard_map/ppermute | solution.py:160
  247.1 0.7 copy.18.requests
  247.7 27.1 %shard_map.78 = f32[2,2,512,512]{3,2,1,0:T(8,128)} custom-call(s32[32,3]{1,0:T(8,128)} %copy.18.requests, f32[1,1]{1,0:T(1,128)} %bitcast.2.peak, f32[32,2,2,128,128]{4,3,2,1,0:T(8,128)} %get-tuple-element.4.terms), custom_call_target="tpu_custom_call" | custom-call | tf_op jit(solution)/shard_map/pallas_call | solution.py:146
  274.8 14.5 %all-reduce.3.cloned.1.call-done = f32[1,2,2,128,128]{4,3,2,1,0:T(8,128)} async-done(((f32[1,2,2,128,128]{4,3,2,1,0:T(8,128)}), f32[1,2,2,128,128]{4,3,2,1,0:T(8,128)}) %all-reduce.3.cloned.1.call-update) | async-done | bytes 262160 | tf_op jit(solution)/shard_map/psum | solution.py:356
  289.3 1.7 copy.25
  (27 shorter events, 3.4 us)
Async XLA Ops:
  7.2 25.0 %copy-start = (bf16[2,2,512,512]{3,2,1,0:T(8,128)(2,1)S(1)}, bf16[2,2,512,512]{3,2,1,0:T(8,128)(2,1)}, u32[]{:S(2)}) copy-start(bf16[2,2,512,512]{3,2,1,0:T(8,128)(2,1)} %param.6) | copy-start | bytes 6291460
  7.2 14.9 %copy-start.1 = (f32[1,16,128,128]{3,2,1,0:T(8,128)S(1)}, f32[1,16,128,128]{3,2,1,0:T(8,128)}, u32[]{:S(2)}) copy-start(f32[1,16,128,128]{3,2,1,0:T(8,128)} %param.9) | copy-start | bytes 3145732
  11.2 13.8 %all-to-all-start = ((s32[8,4,3]{1,2,0:T(4,128)}), s32[8,4,3]{1,2,0:T(4,128)S(1)}, u32[]{:S(2)}, u32[]{:S(2)}) async-start(s32[8,4,3]{1,2,0:T(4,128)} %copy.16), calls=%async_computation | async-start | bytes 32768 | tf_op jit(solution)/shard_map/all_to_all | solution.py:341
  25.0 31.0 %all-to-all-start.1 = ((f32[8,4,128,128]{3,2,1,0:T(8,128)}), f32[8,4,128,128]{3,2,1,0:T(8,128)}, u32[]{:S(2)}, u32[]{:S(2)}) async-start(f32[8,4,128,128]{3,2,1,0:T(8,128)} %bitcast.74), calls=%async_computation.1 | async-start | bytes 4194304 | tf_op jit(solution)/shard_map/all_to_all | solution.py:347
  29.4 259.9 %all-reduce.3.cloned.1.call-start = ((), (), s32[]{:S(2)}) async-start(), calls=%async_computation.2 | async-start | bytes 524288 | tf_op jit(solution)/shard_map/psum | solution.py:356
  56.0 180.1 %copy-start.2 = (f32[1,2,2,128,128]{4,3,2,1,0:T(8,128)S(1)}, f32[1,2,2,128,128]{4,3,2,1,0:T(8,128)}, u32[]{:S(2)}) copy-start(f32[1,2,2,128,128]{4,3,2,1,0:T(8,128)} %param.7) | copy-start | bytes 786436
  236.8 3.8 %collective-permute-start = (f32[]{:T(128)}, f32[]{:T(128)}, u32[]{:S(2)}, u32[]{:S(2)}) collective-permute-start(f32[]{:T(128)} %reduce_max.9), channel_id=1, source_target_pairs={{0,8},{8,0},{16,24},{24,16},{1,9},{9,1},{17,25},{25,17},{2,10},{10... | collective-permute-start | bytes 20 | tf_op jit(solution)/shard_map/ppermute | solution.py:160
  241.8 4.6 %collective-permute-start.1 = (f32[]{:T(128)}, f32[]{:T(128)}, u32[]{:S(2)}, u32[]{:S(2)}) collective-permute-start(f32[]{:T(128)} %max.6), channel_id=1, source_target_pairs={{0,16},{8,24},{16,0},{24,8},{1,17},{9,25},{17,1},{25,9},{2,18},{10... | collective-permute-start | bytes 20 | tf_op jit(solution)/shard_map/ppermute | solution.py:160
Sparse Core Ops, SparseCore 0:
  236.2 53.0 all-reduce.2
where the time goes:
time: 299 us; the launch traced here: 298 us
  Pallas kernels  205 us (69%)
  waiting for transfers between devices  25.1 us (8%)
  matrix products  16.1 us (5%)
  between operations  16 us (5%)
  starting transfers between devices  15.1 us (5%)
  other arithmetic  10.6 us (4%)
  local copies, waits for them, and re-layouts  9.46 us (3%)
    pallas_call x1, Pallas kernels, propagate(): pl.pallas_call(propagate_kernel, grid=(count,), in_specs=[pl.BlockSpec((1...  178 us
    pallas_call x1, Pallas kernels, accumulate(): pl.pallas_call(place_kernel, grid_spec=grid_spec, out_shape=jax.ShapeDtyp...  27.1 us
    dot_general x1, matrix products, cut_windows(): jnp.einsum('kscui,kju->kscij', rows, col_sel, preferred_element_type=jnp....  16.1 us
    psum x1, waiting for transfers between devices, on_device(): probe_grad = lax.psum(adjoint_sum / pos_dev, 'member')[None]  14.5 us
    all_to_all x1, waiting for transfers between devices, on_device(): lax.all_to_all(sent.reshape(members, capacity, patch_side, patch_side), '...  7.71 us
  transfers between devices with their start and end apart: 5, of which 4 were waited for; matrix products, arithmetic and copies ran while one was open for 10% of the time, Pallas kernels for 9%

commit v1 on v0

--- a/solution.py
+++ b/solution.py
@@ -174,48 +174,38 @@
     return high, low
 
 
-def times_right(value, pair):
-    high, low = split_pair(value)
-    return (
-        jnp.dot(high, pair[0], preferred_element_type=jnp.float32)
-        + jnp.dot(low, pair[0], preferred_element_type=jnp.float32)
-        + jnp.dot(high, pair[1], preferred_element_type=jnp.float32)
-    )
-
-
-def times_left(pair, value):
-    high, low = split_pair(value)
-    return (
-        jnp.dot(pair[0], high, preferred_element_type=jnp.float32)
-        + jnp.dot(pair[0], low, preferred_element_type=jnp.float32)
-        + jnp.dot(pair[1], high, preferred_element_type=jnp.float32)
-    )
-
-
-def fourier_2d(real, imag, across, down, inverse):
-    side = real.shape[0]
-    right = times_right(jnp.concatenate([real, imag], axis=0), across)
-    real_c, real_s = right[:side, :side], right[:side, side:]
-    imag_c, imag_s = right[side:, :side], right[side:, side:]
-    if inverse:
-        mid_real, mid_imag = real_c - imag_s, imag_c + real_s
-    else:
-        mid_real, mid_imag = real_c + imag_s, imag_c - real_s
-    left = times_left(down, jnp.concatenate([mid_real, mid_imag], axis=1))
-    c_real, c_imag = left[:side, :side], left[:side, side:]
-    s_real, s_imag = left[side:, :side], left[side:, side:]
-    if inverse:
-        return c_real - s_imag, c_imag + s_real
-    return c_real + s_imag, c_imag - s_real
-
-
-def propagate_kernel(patch_ref, measured_ref, probe_ref, kern_ref, across_ref, down_ref,
+def stack_three(value, axis):
+    high = value.astype(jnp.bfloat16)
+    low = (value - high.astype(jnp.float32)).astype(jnp.bfloat16)
+    return jnp.concatenate([high, low, high], axis=axis)
+
+
+def fourier_2d(fields, right_mat, left_mat):
+    side = fields[0][0].shape[0]
+    count = len(fields)
+    rows = jnp.concatenate([jnp.concatenate([re, im], axis=1) for re, im in fields], axis=0)
+    mid = jnp.dot(stack_three(rows, 1), right_mat, preferred_element_type=jnp.float32)
+    parted = jnp.concatenate(
+        [
+            jnp.concatenate([mid[m * side:(m + 1) * side, :side] for m in range(count)], axis=1),
+            jnp.concatenate([mid[m * side:(m + 1) * side, side:] for m in range(count)], axis=1),
+        ],
+        axis=0,
+    )
+    out = jnp.dot(left_mat, stack_three(parted, 0), preferred_element_type=jnp.float32)
+    return [
+        (out[:side, m * side:(m + 1) * side], out[side:, m * side:(m + 1) * side])
+        for m in range(count)
+    ]
+
+
+def propagate_kernel(patch_ref, measured_ref, probe_ref, kern_ref, mats_right, mats_left,
                      grad_ref, probe_sum_ref):
     slot = pl.program_id(0)
     slice_count = patch_ref.shape[1]
     modes = probe_ref.shape[0]
-    across = (across_ref[0], across_ref[1])
-    down = (down_ref[0], down_ref[1])
+    forward = lambda fields: fourier_2d(fields, mats_right[0], mats_left[0])
+    inverse = lambda fields: fourier_2d(fields, mats_right[1], mats_left[1])
     kern_real, kern_imag = kern_ref[0], kern_ref[1]
     waves = [(probe_ref[m, 0], probe_ref[m, 1]) for m in range(modes)]
     history = []
@@ -229,19 +219,20 @@
             for wr, wi in waves
         ]
         if layer < slice_count - 1:
-            waves = []
-            for lr, li in leaving:
-                fr, fi = fourier_2d(lr, li, across, down, False)
-                tr = kern_real * fr - kern_imag * fi
-                ti = kern_real * fi + kern_imag * fr
-                waves.append(fourier_2d(tr, ti, across, down, True))
-    far = [fourier_2d(lr, li, across, down, False) for lr, li in leaving]
+            spectra = forward(leaving)
+            waves = inverse(
+                [
+                    (kern_real * fr - kern_imag * fi, kern_real * fi + kern_imag * fr)
+                    for fr, fi in spectra
+                ]
+            )
+    far = forward(leaving)
     intensity = None
     for fr, fi in far:
         power = fr * fr + fi * fi
         intensity = power if intensity is None else intensity + power
     factor = 1.0 - measured_ref[0] / jnp.sqrt(jnp.maximum(intensity, 1.0))
-    back = [fourier_2d(fr * factor, fi * factor, across, down, True) for fr, fi in far]
+    back = inverse([(fr * factor, fi * factor) for fr, fi in far])
     for layer in reversed(range(slice_count)):
         grad_real = None
         grad_imag = None
@@ -259,13 +250,13 @@
             for br, bi in back
         ]
         if layer > 0:
-            moved = []
-            for br, bi in back:
-                fr, fi = fourier_2d(br, bi, across, down, False)
-                tr = kern_real * fr + kern_imag * fi
-                ti = kern_real * fi - kern_imag * fr
-                moved.append(fourier_2d(tr, ti, across, down, True))
-            back = moved
+            spectra = forward(back)
+            back = inverse(
+                [
+                    (kern_real * fr + kern_imag * fi, kern_real * fi - kern_imag * fr)
+                    for fr, fi in spectra
+                ]
+            )
 
     @pl.when(slot == 0)
     def _():
@@ -276,21 +267,35 @@
         probe_sum_ref[mode, 1] = probe_sum_ref[mode, 1] + bi
 
 
-def dft_pairs(length):
+def dft_mats(length):
     counter = jnp.arange(length, dtype=jnp.int32)
     product = counter[:, None] * counter[None, :] % length
     angles = product.astype(jnp.float32) * (2.0 * math.pi / length)
     norming = 1.0 / math.sqrt(length)
     cosine = jnp.cos(angles) * norming
     sine = jnp.sin(angles) * norming
-    across = jnp.concatenate([cosine, sine], axis=1)
-    down = jnp.concatenate([cosine, sine], axis=0)
-
-    def pair(value):
+    minus = jnp.concatenate(
+        [jnp.concatenate([cosine, -sine], axis=1), jnp.concatenate([sine, cosine], axis=1)], axis=0
+    )
+    plus = jnp.concatenate(
+        [jnp.concatenate([cosine, sine], axis=1), jnp.concatenate([-sine, cosine], axis=1)], axis=0
+    )
+
+    def parts(value):
         high = lax.reduce_precision(value, exponent_bits=8, mantissa_bits=7)
-        return jnp.stack([high, value - high]).astype(jnp.bfloat16)
-
-    return pair(across), pair(down)
+        return high.astype(jnp.bfloat16), (value - high).astype(jnp.bfloat16)
+
+    def right(value):
+        high, low = parts(value)
+        return jnp.concatenate([high, high, low], axis=0)
+
+    def left(value):
+        high, low = parts(value)
+        return jnp.concatenate([high, high, low], axis=1)
+
+    mats_right = jnp.stack([right(minus), right(plus)])
+    mats_left = jnp.stack([left(plus), left(minus)])
+    return mats_right, mats_left
 
 
 def propagate(patches, measured, probe_modes, prop_phase):
@@ -298,7 +303,7 @@
     modes = probe_modes.shape[0]
     side = patches.shape[-1]
     kern = jnp.stack([jnp.cos(prop_phase), jnp.sin(prop_phase)])
-    across, down = dft_pairs(side)
+    mats_right, mats_left = dft_mats(side)
     whole = lambda shape: pl.BlockSpec(shape, lambda k: (0,) * len(shape))
     return pl.pallas_call(
         propagate_kernel,
@@ -308,8 +313,8 @@
             pl.BlockSpec((1, side, side), lambda k: (k, 0, 0)),
             whole((modes, 2, side, side)),
             whole((2, side, side)),
-            whole((2, side, 2 * side)),
-            whole((2, 2 * side, side)),
+            whole((2, 6 * side, 2 * side)),
+            whole((2, 2 * side, 6 * side)),
         ],
         out_specs=[
             pl.BlockSpec((1, slice_count, 2, side, side), lambda k: (k, 0, 0, 0, 0)),
@@ -320,7 +325,7 @@
             jax.ShapeDtypeStruct((modes, 2, side, side), jnp.float32),
         ],
         compiler_params=pltpu.CompilerParams(dimension_semantics=("arbitrary",)),
-    )(patches, measured, probe_modes, kern, across, down)
+    )(patches, measured, probe_modes, kern, mats_right, mats_left)
 
 
 def on_device(object_field, probe_modes, prop_phase, amplitude, tile_owner, corner):

time: 299 us -> 249 us (0.83)
  Pallas kernels: 205 us -> 156 us
    pallas_call x1, Pallas kernels: 178 us -> 129 us  [propagate(): pl.pallas_call(propagate_kernel, grid=(count,), in_specs=[pl.BlockSpec((1...]
  transfers between devices with their start and end apart: 5 -> 5, of which waited for: 4 -> 4; matrix products, arithmetic and copies ran while one was open for 10% -> 11% of each run, Pallas kernels for 9% -> 11%
where the time goes in v1:
time: 249 us; the launch traced here: 248 us
  Pallas kernels  156 us (63%)
  waiting for transfers between devices  24.8 us (10%)
  matrix products  16.1 us (6%)
  between operations  16.1 us (6%)
  starting transfers between devices  15.3 us (6%)
  other arithmetic  11.1 us (4%)
  local copies, waits for them, and re-layouts  8.62 us (3%)
    pallas_call x1, Pallas kernels, propagate(): pl.pallas_call(propagate_kernel, grid=(count,), in_specs=[pl.BlockSpec((1...  129 us
    pallas_call x1, Pallas kernels, accumulate(): pl.pallas_call(place_kernel, grid_spec=grid_spec, out_shape=jax.ShapeDtyp...  27.1 us
    dot_general x1, matrix products, cut_windows(): jnp.einsum('kscui,kju->kscij', rows, col_sel, preferred_element_type=jnp....  16.1 us
    psum x1, waiting for transfers between devices, on_device(): probe_grad = lax.psum(adjoint_sum / pos_dev, 'member')[None]  14.4 us
    all_to_all x1, waiting for transfers between devices, on_device(): lax.all_to_all(sent.reshape(members, capacity, patch_side, patch_side), '...  7.53 us
    ppermute x2, starting transfers between devices, group_max(): value = jnp.maximum(value, lax.ppermute(value, 'group', pairs))  5.57 us
    all_to_all x1, starting transfers between devices, on_device(): lax.all_to_all(outgoing.reshape(members, capacity, 3), 'member', split_ax...  5.17 us
  transfers between devices with their start and end apart: 5, of which 4 were waited for; matrix products, arithmetic and copies ran while one was open for 11% of the time, Pallas kernels for 11%

profile of v1, /device:TPU:0, one launch (start us, length us, event | category | flops | bytes accessed | tf_op | source)
XLA Modules:
  0.0 247.9 jit_solution(14180323333972212363)
XLA Ops:
  7.2 0.9 fusion.38
  8.1 0.8 select_reduce_fusion
  9.0 0.7 multiply_add_fusion
  9.7 0.7 concatenate.33
  11.2 5.2 %all-to-all-start = ((s32[8,4,3]{1,2,0:T(4,128)}), s32[8,4,3]{1,2,0:T(4,128)S(1)}, u32[]{:S(2)}, u32[]{:S(2)}) async-start(s32[8,4,3]{1,2,0:T(4,128)} %copy.16), calls=%async_computation | async-start | bytes 32768 | tf_op jit(solution)/shard_map/all_to_all | solution.py:346
  17.6 0.9 pad_maximum_fusion.mats_right
  18.5 0.9 pad_maximum_fusion.1.mats_left
  19.5 0.7 pad_maximum_fusion.6.kern_ref
  20.1 1.6 broadcast_in_dim.4
  21.7 2.9 %scatter_fusion = f32[32,128,128]{2,1,0:T(8,128)} fusion(f32[32,128,128]{2,1,0:T(8,128)} %broadcast_in_dim.4, s32[16]{0:T(128)S(1)} %fusion.40, f32[16,128,128]{2,1,0:T(8,128)S(1)} %bitcast.80), kind=kCustom, calls=%fused_computation | custom fusion | bytes 3145792 | tf_op jit(solution)/shard_map/scatter | solution.py:349
  24.7 4.4 %all-to-all-start.1 = ((f32[8,4,128,128]{3,2,1,0:T(8,128)}), f32[8,4,128,128]{3,2,1,0:T(8,128)}, u32[]{:S(2)}, u32[]{:S(2)}) async-start(f32[8,4,128,128]{3,2,1,0:T(8,128)} %bitcast.78), calls=%async_computation.1 | async-start | bytes 4194304 | tf_op jit(solution)/shard_map/all_to_all | solution.py:352
  29.5 2.6 %fusion.55 = pred[32,128,512,1,1]{2,1,4,3,0:T(32,128)(4,1)} fusion(s32[32,128]{1,0:T(8,128)S(1)} %get-tuple-element.14), kind=kLoop, calls=%fused_computation.8.clone.clone.clone.clone.2 | loop fusion | flops 2097152 | bytes 2113536 | tf_op jit(solution)/shard_map/kscui,kju->kscij/dot_general | solution.py:65
  32.1 16.1 %fusion.14.patch_ref = bf16[32,2,2,128,128]{4,3,2,1,0:T(8,128)(2,1)} fusion(s32[32,128]{1,0:T(8,128)S(1)} %get-tuple-element.15, bf16[2,2,512,512]{3,2,1,0:T(8,128)(2,1)S(1)} %copy-done, bf16[32]{0:T(256)(128)(2,1)S(1)} %slice_bitcast_fusion.1, pred[32,128,512,1,1]{2,1,4,3,0:T(32,128)(4,1)} %fusion.55), kind=kOutput, calls=%fused_computation.12 | convolution fusion | flops 10752098304 | bytes 8405056 | tf_op jit(solution)/shard_map/kscui,kju->kscij/dot_general | solution.py:65
  48.2 7.5 %all-to-all-done.1 = f32[8,4,128,128]{3,2,1,0:T(8,128)} async-done(((f32[8,4,128,128]{3,2,1,0:T(8,128)}), f32[8,4,128,128]{3,2,1,0:T(8,128)}, u32[]{:S(2)}, u32[]{:S(2)}) %all-to-all-start.1) | async-done | bytes 2097184 | tf_op jit(solution)/shard_map/all_to_all | solution.py:352
  55.7 128.9 %shard_map.77 = (f32[32,2,2,128,128]{4,3,2,1,0:T(8,128)}, f32[2,2,128,128]{3,2,1,0:T(8,128)}) custom-call(bf16[32,2,2,128,128]{4,3,2,1,0:T(8,128)(2,1)} %fusion.14.patch_ref, f32[32,128,128]{2,1,0:T(8,128)} %bitcast.17.measured_ref, f32[2,2,128,128]{3,2,1,0:T(8,128)} %bitcast.79, f32[2,128,128]{2,1,0:T(8,128)} %pad_maximum_fusion.6.kern_ref, ...), custom_call_target="tpu_custom_call" | custom-call | tf_op jit(solution)/shard_map/pallas_call | solution.py:308
  184.6 1.7 multiply_bitcast_fusion
  186.9 1.6 collective-permute-start
  188.5 2.2 collective-permute-done
  192.0 4.0 %collective-permute-start.1 = (f32[]{:T(128)}, f32[]{:T(128)}, u32[]{:S(2)}, u32[]{:S(2)}) collective-permute-start(f32[]{:T(128)} %max.6), channel_id=1, source_target_pairs={{0,16},{8,24},{16,0},{24,8},{1,17},{9,25},{17,1},{25,9},{2,18},{10... | collective-permute-start | bytes 20 | tf_op jit(solution)/shard_map/ppermute | solution.py:160
  196.0 0.6 collective-permute-done.1
  197.2 0.7 copy.18.requests
  197.9 27.1 %shard_map.78 = f32[2,2,512,512]{3,2,1,0:T(8,128)} custom-call(s32[32,3]{1,0:T(8,128)} %copy.18.requests, f32[1,1]{1,0:T(1,128)} %bitcast.2.peak, f32[32,2,2,128,128]{4,3,2,1,0:T(8,128)} %get-tuple-element.4.terms), custom_call_target="tpu_custom_call" | custom-call | tf_op jit(solution)/shard_map/pallas_call | solution.py:146
  225.0 14.4 %all-reduce.3.cloned.1.call-done = f32[1,2,2,128,128]{4,3,2,1,0:T(8,128)} async-done(((f32[1,2,2,128,128]{4,3,2,1,0:T(8,128)}), f32[1,2,2,128,128]{4,3,2,1,0:T(8,128)}) %all-reduce.3.cloned.1.call-update) | async-done | bytes 262160 | tf_op jit(solution)/shard_map/psum | solution.py:361
  239.4 1.7 copy.25
  (34 shorter events, 3.2 us)
Async XLA Ops:
  7.2 24.9 %copy-start = (bf16[2,2,512,512]{3,2,1,0:T(8,128)(2,1)S(1)}, bf16[2,2,512,512]{3,2,1,0:T(8,128)(2,1)}, u32[]{:S(2)}) copy-start(bf16[2,2,512,512]{3,2,1,0:T(8,128)(2,1)} %param.6) | copy-start | bytes 6291460
  7.2 10.1 %copy-start.4 = (s32[1,16,1]{1,2,0:T(1,128)S(1)}, s32[1,16,1]{1,2,0:T(1,128)}, u32[]{:S(2)}) copy-start(s32[1,16,1]{1,2,0:T(1,128)} %param.10) | copy-start | bytes 196
  7.2 10.1 %copy-start.3 = (f32[128,128]{1,0:T(8,128)S(1)}, f32[128,128]{1,0:T(8,128)}, u32[]{:S(2)}) copy-start(f32[128,128]{1,0:T(8,128)} %param.8) | copy-start | bytes 196612
  11.2 13.5 %all-to-all-start = ((s32[8,4,3]{1,2,0:T(4,128)}), s32[8,4,3]{1,2,0:T(4,128)S(1)}, u32[]{:S(2)}, u32[]{:S(2)}) async-start(s32[8,4,3]{1,2,0:T(4,128)} %copy.16), calls=%async_computation | async-start | bytes 32768 | tf_op jit(solution)/shard_map/all_to_all | solution.py:346
  18.5 3.2 %copy-start.2 = (f32[1,16,128,128]{3,2,1,0:T(8,128)S(1)}, f32[1,16,128,128]{3,2,1,0:T(8,128)}, u32[]{:S(2)}) copy-start(f32[1,16,128,128]{3,2,1,0:T(8,128)} %param.9) | copy-start | bytes 3145732
  24.7 31.0 %all-to-all-start.1 = ((f32[8,4,128,128]{3,2,1,0:T(8,128)}), f32[8,4,128,128]{3,2,1,0:T(8,128)}, u32[]{:S(2)}, u32[]{:S(2)}) async-start(f32[8,4,128,128]{3,2,1,0:T(8,128)} %bitcast.78), calls=%async_computation.1 | async-start | bytes 4194304 | tf_op jit(solution)/shard_map/all_to_all | solution.py:352
  29.1 210.4 %all-reduce.3.cloned.1.call-start = ((), (), s32[]{:S(2)}) async-start(), calls=%async_computation.2 | async-start | bytes 524288 | tf_op jit(solution)/shard_map/psum | solution.py:361
  55.7 130.6 %copy-start.1 = (f32[1,2,2,128,128]{4,3,2,1,0:T(8,128)S(1)}, f32[1,2,2,128,128]{4,3,2,1,0:T(8,128)}, u32[]{:S(2)}) copy-start(f32[1,2,2,128,128]{4,3,2,1,0:T(8,128)} %param.7) | copy-start | bytes 786436
  186.9 3.8 %collective-permute-start = (f32[]{:T(128)}, f32[]{:T(128)}, u32[]{:S(2)}, u32[]{:S(2)}) collective-permute-start(f32[]{:T(128)} %reduce_max.9), channel_id=1, source_target_pairs={{0,8},{8,0},{16,24},{24,16},{1,9},{9,1},{17,25},{25,17},{2,10},{10... | collective-permute-start | bytes 20 | tf_op jit(solution)/shard_map/ppermute | solution.py:160
  192.0 4.6 %collective-permute-start.1 = (f32[]{:T(128)}, f32[]{:T(128)}, u32[]{:S(2)}, u32[]{:S(2)}) collective-permute-start(f32[]{:T(128)} %max.6), channel_id=1, source_target_pairs={{0,16},{8,24},{16,0},{24,8},{1,17},{9,25},{17,1},{25,9},{2,18},{10... | collective-permute-start | bytes 20 | tf_op jit(solution)/shard_map/ppermute | solution.py:160
Sparse Core Ops, SparseCore 0:
  186.4 52.9 all-reduce.2

commit v2 on v1

--- a/solution.py
+++ b/solution.py
@@ -200,8 +200,18 @@
 
 
 def propagate_kernel(patch_ref, measured_ref, probe_ref, kern_ref, mats_right, mats_left,
-                     grad_ref, probe_sum_ref):
-    slot = pl.program_id(0)
+                     peak_ref, grad_ref, probe_sum_ref):
+    @pl.when(pl.program_id(0) == 0)
+    def _():
+        probe_sum_ref[...] = jnp.zeros_like(probe_sum_ref)
+
+    for held in range(patch_ref.shape[0]):
+        propagate_one(held, patch_ref, measured_ref, probe_ref, kern_ref, mats_right, mats_left,
+                      grad_ref, probe_sum_ref)
+
+
+def propagate_one(held, patch_ref, measured_ref, probe_ref, kern_ref, mats_right, mats_left,
+                  grad_ref, probe_sum_ref):
     slice_count = patch_ref.shape[1]
     modes = probe_ref.shape[0]
     forward = lambda fields: fourier_2d(fields, mats_right[0], mats_left[0])
@@ -212,8 +222,8 @@
     leaving = None
     for layer in range(slice_count):
         history.append(waves)
-        patch_real = patch_ref[0, layer, 0].astype(jnp.float32)
-        patch_imag = patch_ref[0, layer, 1].astype(jnp.float32)
+        patch_real = patch_ref[held, layer, 0].astype(jnp.float32)
+        patch_imag = patch_ref[held, layer, 1].astype(jnp.float32)
         leaving = [
             (wr * patch_real - wi * patch_imag, wr * patch_imag + wi * patch_real)
             for wr, wi in waves
@@ -231,7 +241,7 @@
     for fr, fi in far:
         power = fr * fr + fi * fi
         intensity = power if intensity is None else intensity + power
-    factor = 1.0 - measured_ref[0] / jnp.sqrt(jnp.maximum(intensity, 1.0))
+    factor = 1.0 - measured_ref[held] / jnp.sqrt(jnp.maximum(intensity, 1.0))
     back = inverse([(fr * factor, fi * factor) for fr, fi in far])
     for layer in reversed(range(slice_count)):
         grad_real = None
@@ -241,10 +251,10 @@
             term_imag = wr * bi - wi * br
             grad_real = term_real if grad_real is None else grad_real + term_real
             grad_imag = term_imag if grad_imag is None else grad_imag + term_imag
-        grad_ref[0, layer, 0] = grad_real
-        grad_ref[0, layer, 1] = grad_imag
-        patch_real = patch_ref[0, layer, 0].astype(jnp.float32)
-        patch_imag = patch_ref[0, layer, 1].astype(jnp.float32)
+        grad_ref[held, layer, 0] = grad_real
+        grad_ref[held, layer, 1] = grad_imag
+        patch_real = patch_ref[held, layer, 0].astype(jnp.float32)
+        patch_imag = patch_ref[held, layer, 1].astype(jnp.float32)
         back = [
             (patch_real * br + patch_imag * bi, patch_real * bi - patch_imag * br)
             for br, bi in back
@@ -258,10 +268,6 @@
                 ]
             )
 
-    @pl.when(slot == 0)
-    def _():
-        probe_sum_ref[...] = jnp.zeros_like(probe_sum_ref)
-
     for mode, (br, bi) in enumerate(back):
         probe_sum_ref[mode, 0] = probe_sum_ref[mode, 0] + br
         probe_sum_ref[mode, 1] = probe_sum_ref[mode, 1] + bi
@@ -298,26 +304,28 @@
     return mats_right, mats_left
 
 
-def propagate(patches, measured, probe_modes, prop_phase):
+def propagate(patches, measured, probe_modes, prop_phase, peak):
     count, slice_count = patches.shape[:2]
     modes = probe_modes.shape[0]
     side = patches.shape[-1]
     kern = jnp.stack([jnp.cos(prop_phase), jnp.sin(prop_phase)])
     mats_right, mats_left = dft_mats(side)
+    held = 2 if count % 2 == 0 else 1
     whole = lambda shape: pl.BlockSpec(shape, lambda k: (0,) * len(shape))
     return pl.pallas_call(
         propagate_kernel,
-        grid=(count,),
+        grid=(count // held,),
         in_specs=[
-            pl.BlockSpec((1, slice_count, 2, side, side), lambda k: (k, 0, 0, 0, 0)),
-            pl.BlockSpec((1, side, side), lambda k: (k, 0, 0)),
+            pl.BlockSpec((held, slice_count, 2, side, side), lambda k: (k, 0, 0, 0, 0)),
+            pl.BlockSpec((held, side, side), lambda k: (k, 0, 0)),
             whole((modes, 2, side, side)),
             whole((2, side, side)),
             whole((2, 6 * side, 2 * side)),
             whole((2, 2 * side, 6 * side)),
+            pl.BlockSpec(memory_space=pltpu.SMEM),
         ],
         out_specs=[
-            pl.BlockSpec((1, slice_count, 2, side, side), lambda k: (k, 0, 0, 0, 0)),
+            pl.BlockSpec((held, slice_count, 2, side, side), lambda k: (k, 0, 0, 0, 0)),
             whole((modes, 2, side, side)),
         ],
         out_shape=[
@@ -325,7 +333,16 @@
             jax.ShapeDtypeStruct((modes, 2, side, side), jnp.float32),
         ],
         compiler_params=pltpu.CompilerParams(dimension_semantics=("arbitrary",)),
-    )(patches, measured, probe_modes, kern, mats_right, mats_left)
+    )(patches, measured, probe_modes, kern, mats_right, mats_left, peak.reshape(1, 1))
+
+
+def member_sum(value, members):
+    flat = value.reshape(members, -1)
+    pieces = lax.all_to_all(flat, "member", split_axis=0, concat_axis=0, tiled=True)
+    mine = jnp.sum(pieces, axis=0, keepdims=True)
+    spread = jnp.broadcast_to(mine, flat.shape)
+    whole = lax.all_to_all(spread, "member", split_axis=0, concat_axis=0, tiled=True)
+    return whole.reshape(value.shape)
 
 
 def on_device(object_field, probe_modes, prop_phase, amplitude, tile_owner, corner):
@@ -357,8 +374,8 @@
         tiled=True,
     ).reshape(slot_count, patch_side, patch_side)
     patches = cut_windows(object_field, requests, patch_side)
-    gradients, adjoint_sum = propagate(patches, measured, probe_modes[0], prop_phase)
-    probe_grad = lax.psum(adjoint_sum / pos_dev, "member")[None]
+    gradients, adjoint_sum = propagate(patches, measured, probe_modes[0], prop_phase, peak_power)
+    probe_grad = member_sum(adjoint_sum / pos_dev, members)[None]
     object_grad = accumulate(gradients, requests, peak_power, tile_cells)
     return (object_grad, probe_grad)
 

time: 249 us -> 223 us (0.90)
  waiting for transfers between devices: 24.8 us -> 8.22 us
  between operations: 16.1 us -> 2.67 us
  blocking collectives: 0 us -> 9.35 us
  Pallas kernels: 156 us -> 147 us
  starting transfers between devices: 15.3 us -> 18.7 us
    psum x1 -> x0, waiting for transfers between devices: 14.4 us -> none  [on_device(): probe_grad = lax.psum(adjoint_sum / pos_dev, 'member')[None]]
    all_to_all x0 -> x1, blocking collectives: none -> 9.35 us  [member_sum(): lax.all_to_all(flat, 'member', split_axis=0, concat_axis=0, tiled=True)]
    pallas_call x1, Pallas kernels: 129 us -> 120 us  [propagate(): pl.pallas_call(propagate_kernel, grid=(count // held,), in_specs=[pl.Bloc...]
    all_to_all x0 -> x1, starting transfers between devices: none -> 3.41 us  [member_sum(): lax.all_to_all(spread, 'member', split_axis=0, concat_axis=0, tiled=True)]
  transfers between devices with their start and end apart: 5 -> 5, of which waited for: 4 -> 2; matrix products, arithmetic and copies ran while one was open for 11% -> 13% of each run, Pallas kernels for 11% -> 12%
where the time goes in v2:
time: 223 us; the launch traced here: 222 us
  Pallas kernels  147 us (66%)
  starting transfers between devices  18.7 us (8%)
  matrix products  16.1 us (7%)
  other arithmetic  11.5 us (5%)
  blocking collectives  9.35 us (4%)
  local copies, waits for them, and re-layouts  8.52 us (4%)
  waiting for transfers between devices  8.22 us (4%)
  between operations  2.67 us (1%)
    pallas_call x1, Pallas kernels, propagate(): pl.pallas_call(propagate_kernel, grid=(count // held,), in_specs=[pl.Bloc...  120 us
    pallas_call x1, Pallas kernels, accumulate(): pl.pallas_call(place_kernel, grid_spec=grid_spec, out_shape=jax.ShapeDtyp...  27 us
    dot_general x1, matrix products, cut_windows(): jnp.einsum('kscui,kju->kscij', rows, col_sel, preferred_element_type=jnp....  16.1 us
    all_to_all x1, blocking collectives, member_sum(): lax.all_to_all(flat, 'member', split_axis=0, concat_axis=0, tiled=True)  9.35 us
    all_to_all x1, waiting for transfers between devices, on_device(): lax.all_to_all(sent.reshape(members, capacity, patch_side, patch_side), '...  7.57 us
    ppermute x2, starting transfers between devices, group_max(): value = jnp.maximum(value, lax.ppermute(value, 'group', pairs))  5.54 us
    all_to_all x1, starting transfers between devices, on_device(): lax.all_to_all(outgoing.reshape(members, capacity, 3), 'member', split_ax...  5.17 us
    all_to_all x1, starting transfers between devices, on_device(): lax.all_to_all(sent.reshape(members, capacity, patch_side, patch_side), '...  4.55 us
  transfers between devices with their start and end apart: 5, of which 2 were waited for; matrix products, arithmetic and copies ran while one was open for 13% of the time, Pallas kernels for 12%

profile of v2, /device:TPU:0, one launch (start us, length us, event | category | flops | bytes accessed | tf_op | source)
XLA Modules:
  0.0 222.1 jit_solution(17259007212341874860)
XLA Ops:
  0.7 0.9 fusion.38
  1.6 0.8 select_reduce_fusion
  2.4 0.7 multiply_add_fusion
  3.2 0.7 concatenate.33
  4.6 5.2 %all-to-all-start = ((s32[8,4,3]{1,2,0:T(4,128)}), s32[8,4,3]{1,2,0:T(4,128)S(1)}, u32[]{:S(2)}, u32[]{:S(2)}) async-start(s32[8,4,3]{1,2,0:T(4,128)} %copy.17), calls=%async_computation | async-start | bytes 32768 | tf_op jit(solution)/shard_map/all_to_all | solution.py:363
  9.8 1.0 multiply_reduce_fusion
  11.4 1.6 collective-permute-start
  14.2 1.0 pad_maximum_fusion.mats_right
  15.2 0.9 pad_maximum_fusion.1.mats_left
  16.8 1.6 broadcast_in_dim.4
  18.4 3.0 %scatter_fusion = f32[32,128,128]{2,1,0:T(8,128)} fusion(f32[32,128,128]{2,1,0:T(8,128)} %broadcast_in_dim.4, s32[16]{0:T(128)S(1)} %fusion.40, f32[16,128,128]{2,1,0:T(8,128)S(1)} %bitcast.80), kind=kCustom, calls=%fused_computation | custom fusion | bytes 3145792 | tf_op jit(solution)/shard_map/scatter | solution.py:366
  22.6 4.0 %collective-permute-start.1 = (f32[]{:T(128)}, f32[]{:T(128)}, u32[]{:S(2)}, u32[]{:S(2)}) collective-permute-start(f32[]{:T(128)} %max.6), channel_id=1, source_target_pairs={{0,16},{8,24},{16,0},{24,8},{1,17},{9,25},{17,1},{25,9},{2,18},{10... | collective-permute-start | bytes 20 | tf_op jit(solution)/shard_map/ppermute | solution.py:160
  27.8 4.5 %all-to-all-start.1 = ((f32[8,4,128,128]{3,2,1,0:T(8,128)}), f32[8,4,128,128]{3,2,1,0:T(8,128)}, u32[]{:S(2)}, u32[]{:S(2)}) async-start(f32[8,4,128,128]{3,2,1,0:T(8,128)} %bitcast.78), calls=%async_computation.1 | async-start | bytes 4194304 | tf_op jit(solution)/shard_map/all_to_all | solution.py:369
  32.6 2.6 %fusion.55 = pred[32,128,512,1,1]{2,1,4,3,0:T(32,128)(4,1)} fusion(s32[32,128]{1,0:T(8,128)S(1)} %get-tuple-element.14), kind=kLoop, calls=%fused_computation.8.clone.clone.clone.clone.2 | loop fusion | flops 2097152 | bytes 2113536 | tf_op jit(solution)/shard_map/kscui,kju->kscij/dot_general | solution.py:65
  35.2 16.1 %fusion.14.patch_ref = bf16[32,2,2,128,128]{4,3,2,1,0:T(8,128)(2,1)} fusion(s32[32,128]{1,0:T(8,128)S(1)} %get-tuple-element.15, bf16[2,2,512,512]{3,2,1,0:T(8,128)(2,1)S(1)} %copy-done, bf16[32]{0:T(256)(128)(2,1)S(1)} %slice_bitcast_fusion.1, pred[32,128,512,1,1]{2,1,4,3,0:T(32,128)(4,1)} %fusion.55), kind=kOutput, calls=%fused_computation.12 | convolution fusion | flops 10752098304 | bytes 8405056 | tf_op jit(solution)/shard_map/kscui,kju->kscij/dot_general | solution.py:65
  51.3 7.6 %all-to-all-done.1 = f32[8,4,128,128]{3,2,1,0:T(8,128)} async-done(((f32[8,4,128,128]{3,2,1,0:T(8,128)}), f32[8,4,128,128]{3,2,1,0:T(8,128)}, u32[]{:S(2)}, u32[]{:S(2)}) %all-to-all-start.1) | async-done | bytes 2097184 | tf_op jit(solution)/shard_map/all_to_all | solution.py:369
  58.9 120.1 %shard_map.77 = (f32[32,2,2,128,128]{4,3,2,1,0:T(8,128)}, f32[2,2,128,128]{3,2,1,0:T(8,128)}) custom-call(bf16[32,2,2,128,128]{4,3,2,1,0:T(8,128)(2,1)} %fusion.14.patch_ref, f32[32,128,128]{2,1,0:T(8,128)} %bitcast.17.measured_ref, f32[2,2,128,128]{3,2,1,0:T(8,128)} %bitcast.79, f32[2,128,128]{2,1,0:T(8,128)} %pad_maximum_fusion.6.kern_ref, ...), custom_call_target="tpu_custom_call" | custom-call | tf_op jit(solution)/shard_map/pallas_call | solution.py:315
  178.9 1.0 broadcast_multiply_fusion
  179.9 9.3 %all_to_all.25 = f32[8,1,8192]{2,1,0:T(1,128)S(1)} all-to-all(f32[8,1,8192]{2,1,0:T(1,128)S(1)} %bitcast.82), channel_id=1, replica_groups=mesh['group'=4,'member'=8] {'member'}, dimensions={0} | all-to-all | bytes 524288 | tf_op jit(solution)/shard_map/all_to_all | solution.py:341
  189.4 0.8 broadcast_in_dim.5
  190.3 3.4 %all-to-all-start.3 = ((f32[8,1,8192]{2,1,0:T(1,128)}), f32[8,1,8192]{2,1,0:T(1,128)S(1)}, u32[]{:S(2)}, u32[]{:S(2)}) async-start(f32[8,1,8192]{2,1,0:T(1,128)} %broadcast_in_dim.5), calls=%async_computation.3 | async-start | bytes 524288 | tf_op jit(solution)/shard_map/all_to_all | solution.py:344
  193.7 0.7 copy.19.requests
  194.4 27.0 %shard_map.78 = f32[2,2,512,512]{3,2,1,0:T(8,128)} custom-call(s32[32,3]{1,0:T(8,128)} %copy.19.requests, f32[1,1]{1,0:T(1,128)} %bitcast.2.peak_ref.peak, f32[32,2,2,128,128]{4,3,2,1,0:T(8,128)} %get-tuple-element.4.terms), custom_call_target="tpu_custom_call" | custom-call | tf_op jit(solution)/shard_map/pallas_call | solution.py:146
  221.4 0.7 copy.27
  (34 shorter events, 4.4 us)
Async XLA Ops:
  0.6 34.6 %copy-start = (bf16[2,2,512,512]{3,2,1,0:T(8,128)(2,1)S(1)}, bf16[2,2,512,512]{3,2,1,0:T(8,128)(2,1)}, u32[]{:S(2)}) copy-start(bf16[2,2,512,512]{3,2,1,0:T(8,128)(2,1)} %param.6) | copy-start | bytes 6291460
  0.6 13.3 %copy-start.3 = (s32[1,16,1]{1,2,0:T(1,128)S(1)}, s32[1,16,1]{1,2,0:T(1,128)}, u32[]{:S(2)}) copy-start(s32[1,16,1]{1,2,0:T(1,128)} %param.10) | copy-start | bytes 196
  0.7 13.3 %copy-start.2 = (f32[128,128]{1,0:T(8,128)S(1)}, f32[128,128]{1,0:T(8,128)}, u32[]{:S(2)}) copy-start(f32[128,128]{1,0:T(8,128)} %param.8) | copy-start | bytes 196612
  4.6 23.2 %all-to-all-start = ((s32[8,4,3]{1,2,0:T(4,128)}), s32[8,4,3]{1,2,0:T(4,128)S(1)}, u32[]{:S(2)}, u32[]{:S(2)}) async-start(s32[8,4,3]{1,2,0:T(4,128)} %copy.17), calls=%async_computation | async-start | bytes 32768 | tf_op jit(solution)/shard_map/all_to_all | solution.py:363
  11.4 9.9 %collective-permute-start = (f32[]{:T(128)}, f32[]{:T(128)}, u32[]{:S(2)}, u32[]{:S(2)}) collective-permute-start(f32[]{:T(128)} %reduce_max.9), channel_id=1, source_target_pairs={{0,8},{8,0},{16,24},{24,16},{1,9},{9,1},{17,25},{25,17},{2,10},{10... | collective-permute-start | bytes 20 | tf_op jit(solution)/shard_map/ppermute | solution.py:160
  15.2 3.2 %copy-start.1 = (f32[1,16,128,128]{3,2,1,0:T(8,128)S(1)}, f32[1,16,128,128]{3,2,1,0:T(8,128)}, u32[]{:S(2)}) copy-start(f32[1,16,128,128]{3,2,1,0:T(8,128)} %param.9) | copy-start | bytes 3145732
  22.6 4.6 %collective-permute-start.1 = (f32[]{:T(128)}, f32[]{:T(128)}, u32[]{:S(2)}, u32[]{:S(2)}) collective-permute-start(f32[]{:T(128)} %max.6), channel_id=1, source_target_pairs={{0,16},{8,24},{16,0},{24,8},{1,17},{9,25},{17,1},{25,9},{2,18},{10... | collective-permute-start | bytes 20 | tf_op jit(solution)/shard_map/ppermute | solution.py:160
  27.8 31.0 %all-to-all-start.1 = ((f32[8,4,128,128]{3,2,1,0:T(8,128)}), f32[8,4,128,128]{3,2,1,0:T(8,128)}, u32[]{:S(2)}, u32[]{:S(2)}) async-start(f32[8,4,128,128]{3,2,1,0:T(8,128)} %bitcast.78), calls=%async_computation.1 | async-start | bytes 4194304 | tf_op jit(solution)/shard_map/all_to_all | solution.py:369
  190.3 31.1 %all-to-all-start.3 = ((f32[8,1,8192]{2,1,0:T(1,128)}), f32[8,1,8192]{2,1,0:T(1,128)S(1)}, u32[]{:S(2)}, u32[]{:S(2)}) async-start(f32[8,1,8192]{2,1,0:T(1,128)} %broadcast_in_dim.5), calls=%async_computation.3 | async-start | bytes 524288 | tf_op jit(solution)/shard_map/all_to_all | solution.py:344

commit v3 on v2

--- a/solution.py
+++ b/solution.py
@@ -67,15 +67,25 @@
 
 
 def place_kernel(requests, peak, terms, out, total):
-    slot = pl.program_id(0)
+    step = pl.program_id(0)
+    held = terms.shape[0]
+    tile_cells = out.shape[-1]
+
+    @pl.when(step == 0)
+    def _():
+        total[...] = jnp.zeros_like(total)
+
+    for index in range(held):
+        place_one(step * held + index, index, requests, terms, total)
+
+    @pl.when(step == pl.num_programs(0) - 1)
+    def _():
+        out[...] = total[:, :, :tile_cells, :tile_cells] / peak[0, 0]
+
+
+def place_one(slot, index, requests, terms, total):
     slice_count = terms.shape[1]
     patch_side = terms.shape[-1]
-    tile_cells = out.shape[-1]
-
-    @pl.when(slot == 0)
-    def _():
-        total[...] = jnp.zeros_like(total)
-
     row = requests[slot, 1]
     col = requests[slot, 2]
     row_base = pl.multiple_of((row // 8) * 8, 8)
@@ -95,7 +105,7 @@
     pieces = []
     for layer in range(slice_count):
         for part in range(2):
-            term = terms[0, layer, part]
+            term = terms[index, layer, part]
             high = term.astype(jnp.bfloat16)
             low = (term - high.astype(jnp.float32)).astype(jnp.bfloat16)
             pieces += [high, low]
@@ -117,21 +127,18 @@
             window = total.at[layer, part, pl.ds(row_base, band_rows), pl.ds(col_base, band_cols)]
             window[...] = window[...] + band
 
-    @pl.when(slot == pl.num_programs(0) - 1)
-    def _():
-        out[...] = total[:, :, :tile_cells, :tile_cells] / peak[0, 0]
-
 
 def accumulate(terms, requests, peak, tile_cells):
     slot_count, slice_count = terms.shape[:2]
     patch_side = terms.shape[-1]
+    held = math.gcd(slot_count, 4)
     grid_spec = pltpu.PrefetchScalarGridSpec(
         num_scalar_prefetch=1,
-        grid=(slot_count,),
+        grid=(slot_count // held,),
         in_specs=[
             pl.BlockSpec(memory_space=pltpu.SMEM),
             pl.BlockSpec(
-                (1, slice_count, 2, patch_side, patch_side), lambda k, req: (k, 0, 0, 0, 0)
+                (held, slice_count, 2, patch_side, patch_side), lambda k, req: (k, 0, 0, 0, 0)
             ),
         ],
         out_specs=pl.BlockSpec(
@@ -310,7 +317,7 @@
     side = patches.shape[-1]
     kern = jnp.stack([jnp.cos(prop_phase), jnp.sin(prop_phase)])
     mats_right, mats_left = dft_mats(side)
-    held = 2 if count % 2 == 0 else 1
+    held = math.gcd(count, 4)
     whole = lambda shape: pl.BlockSpec(shape, lambda k: (0,) * len(shape))
     return pl.pallas_call(
         propagate_kernel,

time: 223 us -> 207 us (0.928)
  Pallas kernels: 147 us -> 131 us
    pallas_call x1, Pallas kernels: 27 us -> 14.5 us  [accumulate(): pl.pallas_call(place_kernel, grid_spec=grid_spec, out_shape=jax.ShapeDtyp...]
    pallas_call x1, Pallas kernels: 120 us -> 116 us  [propagate(): pl.pallas_call(propagate_kernel, grid=(count // held,), in_specs=[pl.Bloc...]
  transfers between devices with their start and end apart: 5 -> 5, of which waited for: 2 -> 2; matrix products, arithmetic and copies ran while one was open for 13% -> 14% of each run, Pallas kernels for 12% -> 7%
where the time goes in v3:
time: 207 us; the launch traced here: 206 us
  Pallas kernels  131 us (63%)
  starting transfers between devices  18.5 us (9%)
  matrix products  16.1 us (8%)
  other arithmetic  11.5 us (6%)
  blocking collectives  9.35 us (5%)
  local copies, waits for them, and re-layouts  8.54 us (4%)
  waiting for transfers between devices  8.41 us (4%)
  between operations  2.67 us (1%)
    pallas_call x1, Pallas kernels, propagate(): pl.pallas_call(propagate_kernel, grid=(count // held,), in_specs=[pl.Bloc...  116 us
    dot_general x1, matrix products, cut_windows(): jnp.einsum('kscui,kju->kscij', rows, col_sel, preferred_element_type=jnp....  16.1 us
    pallas_call x1, Pallas kernels, accumulate(): pl.pallas_call(place_kernel, grid_spec=grid_spec, out_shape=jax.ShapeDtyp...  14.5 us
    all_to_all x1, blocking collectives, member_sum(): lax.all_to_all(flat, 'member', split_axis=0, concat_axis=0, tiled=True)  9.35 us
    all_to_all x1, waiting for transfers between devices, on_device(): lax.all_to_all(sent.reshape(members, capacity, patch_side, patch_side), '...  7.75 us
    ppermute x2, starting transfers between devices, group_max(): value = jnp.maximum(value, lax.ppermute(value, 'group', pairs))  5.53 us
    all_to_all x1, starting transfers between devices, on_device(): lax.all_to_all(outgoing.reshape(members, capacity, 3), 'member', split_ax...  5.17 us
    all_to_all x1, starting transfers between devices, on_device(): lax.all_to_all(sent.reshape(members, capacity, patch_side, patch_side), '...  4.37 us
  transfers between devices with their start and end apart: 5, of which 2 were waited for; matrix products, arithmetic and copies ran while one was open for 14% of the time, Pallas kernels for 7%

profile of v3, /device:TPU:0, one launch (start us, length us, event | category | flops | bytes accessed | tf_op | source)
XLA Modules:
  0.0 206.0 jit_solution(9859787287476676194)
XLA Ops:
  0.7 0.9 fusion.38
  1.6 0.8 select_reduce_fusion
  2.4 0.7 multiply_add_fusion
  3.2 0.7 concatenate.33
  4.6 5.2 %all-to-all-start = ((s32[8,4,3]{1,2,0:T(4,128)}), s32[8,4,3]{1,2,0:T(4,128)S(1)}, u32[]{:S(2)}, u32[]{:S(2)}) async-start(s32[8,4,3]{1,2,0:T(4,128)} %copy.17), calls=%async_computation | async-start | bytes 32768 | tf_op jit(solution)/shard_map/all_to_all | solution.py:370
  9.8 1.0 multiply_reduce_fusion
  11.4 1.6 collective-permute-start
  14.2 1.0 pad_maximum_fusion.mats_right
  15.2 0.9 pad_maximum_fusion.1.mats_left
  16.8 1.6 broadcast_in_dim.4
  18.4 3.0 %scatter_fusion = f32[32,128,128]{2,1,0:T(8,128)} fusion(f32[32,128,128]{2,1,0:T(8,128)} %broadcast_in_dim.4, s32[16]{0:T(128)S(1)} %fusion.40, f32[16,128,128]{2,1,0:T(8,128)S(1)} %bitcast.80), kind=kCustom, calls=%fused_computation | custom fusion | bytes 3145792 | tf_op jit(solution)/shard_map/scatter | solution.py:373
  22.6 4.0 %collective-permute-start.1 = (f32[]{:T(128)}, f32[]{:T(128)}, u32[]{:S(2)}, u32[]{:S(2)}) collective-permute-start(f32[]{:T(128)} %max.6), channel_id=1, source_target_pairs={{0,16},{8,24},{16,0},{24,8},{1,17},{9,25},{17,1},{25,9},{2,18},{10... | collective-permute-start | bytes 20 | tf_op jit(solution)/shard_map/ppermute | solution.py:167
  27.9 4.4 %all-to-all-start.1 = ((f32[8,4,128,128]{3,2,1,0:T(8,128)}), f32[8,4,128,128]{3,2,1,0:T(8,128)}, u32[]{:S(2)}, u32[]{:S(2)}) async-start(f32[8,4,128,128]{3,2,1,0:T(8,128)} %bitcast.78), calls=%async_computation.1 | async-start | bytes 4194304 | tf_op jit(solution)/shard_map/all_to_all | solution.py:376
  32.4 2.6 %fusion.55 = pred[32,128,512,1,1]{2,1,4,3,0:T(32,128)(4,1)} fusion(s32[32,128]{1,0:T(8,128)S(1)} %get-tuple-element.14), kind=kLoop, calls=%fused_computation.8.clone.clone.clone.clone.2 | loop fusion | flops 2097152 | bytes 2113536 | tf_op jit(solution)/shard_map/kscui,kju->kscij/dot_general | solution.py:65
  35.1 16.1 %fusion.14.patch_ref = bf16[32,2,2,128,128]{4,3,2,1,0:T(8,128)(2,1)} fusion(s32[32,128]{1,0:T(8,128)S(1)} %get-tuple-element.15, bf16[2,2,512,512]{3,2,1,0:T(8,128)(2,1)S(1)} %copy-done, bf16[32]{0:T(256)(128)(2,1)S(1)} %slice_bitcast_fusion.1, pred[32,128,512,1,1]{2,1,4,3,0:T(32,128)(4,1)} %fusion.55), kind=kOutput, calls=%fused_computation.12 | convolution fusion | flops 10752098304 | bytes 8405056 | tf_op jit(solution)/shard_map/kscui,kju->kscij/dot_general | solution.py:65
  51.1 7.8 %all-to-all-done.1 = f32[8,4,128,128]{3,2,1,0:T(8,128)} async-done(((f32[8,4,128,128]{3,2,1,0:T(8,128)}), f32[8,4,128,128]{3,2,1,0:T(8,128)}, u32[]{:S(2)}, u32[]{:S(2)}) %all-to-all-start.1) | async-done | bytes 2097184 | tf_op jit(solution)/shard_map/all_to_all | solution.py:376
  58.9 116.4 %shard_map.77 = (f32[32,2,2,128,128]{4,3,2,1,0:T(8,128)}, f32[2,2,128,128]{3,2,1,0:T(8,128)}) custom-call(bf16[32,2,2,128,128]{4,3,2,1,0:T(8,128)(2,1)} %fusion.14.patch_ref, f32[32,128,128]{2,1,0:T(8,128)} %bitcast.17.measured_ref, f32[2,2,128,128]{3,2,1,0:T(8,128)} %bitcast.79, f32[2,128,128]{2,1,0:T(8,128)} %pad_maximum_fusion.6.kern_ref, ...), custom_call_target="tpu_custom_call" | custom-call | tf_op jit(solution)/shard_map/pallas_call | solution.py:322
  175.3 1.0 broadcast_multiply_fusion
  176.2 9.3 %all_to_all.25 = f32[8,1,8192]{2,1,0:T(1,128)S(1)} all-to-all(f32[8,1,8192]{2,1,0:T(1,128)S(1)} %bitcast.82), channel_id=1, replica_groups=mesh['group'=4,'member'=8] {'member'}, dimensions={0} | all-to-all | bytes 524288 | tf_op jit(solution)/shard_map/all_to_all | solution.py:348
  185.8 0.8 broadcast_in_dim.5
  186.6 3.4 %all-to-all-start.3 = ((f32[8,1,8192]{2,1,0:T(1,128)}), f32[8,1,8192]{2,1,0:T(1,128)S(1)}, u32[]{:S(2)}, u32[]{:S(2)}) async-start(f32[8,1,8192]{2,1,0:T(1,128)} %broadcast_in_dim.5), calls=%async_computation.3 | async-start | bytes 524288 | tf_op jit(solution)/shard_map/all_to_all | solution.py:351
  190.1 0.7 copy.19.requests
  190.7 14.5 %shard_map.78 = f32[2,2,512,512]{3,2,1,0:T(8,128)} custom-call(s32[32,3]{1,0:T(8,128)} %copy.19.requests, f32[1,1]{1,0:T(1,128)} %bitcast.2.peak_ref.peak, f32[32,2,2,128,128]{4,3,2,1,0:T(8,128)} %get-tuple-element.4.terms), custom_call_target="tpu_custom_call" | custom-call | tf_op jit(solution)/shard_map/pallas_call | solution.py:153
  205.2 0.7 copy.27
  (34 shorter events, 4.4 us)
Async XLA Ops:
  0.6 34.4 %copy-start = (bf16[2,2,512,512]{3,2,1,0:T(8,128)(2,1)S(1)}, bf16[2,2,512,512]{3,2,1,0:T(8,128)(2,1)}, u32[]{:S(2)}) copy-start(bf16[2,2,512,512]{3,2,1,0:T(8,128)(2,1)} %param.6) | copy-start | bytes 6291460
  0.6 13.3 %copy-start.3 = (s32[1,16,1]{1,2,0:T(1,128)S(1)}, s32[1,16,1]{1,2,0:T(1,128)}, u32[]{:S(2)}) copy-start(s32[1,16,1]{1,2,0:T(1,128)} %param.10) | copy-start | bytes 196
  0.7 13.3 %copy-start.2 = (f32[128,128]{1,0:T(8,128)S(1)}, f32[128,128]{1,0:T(8,128)}, u32[]{:S(2)}) copy-start(f32[128,128]{1,0:T(8,128)} %param.8) | copy-start | bytes 196612
  4.6 23.2 %all-to-all-start = ((s32[8,4,3]{1,2,0:T(4,128)}), s32[8,4,3]{1,2,0:T(4,128)S(1)}, u32[]{:S(2)}, u32[]{:S(2)}) async-start(s32[8,4,3]{1,2,0:T(4,128)} %copy.17), calls=%async_computation | async-start | bytes 32768 | tf_op jit(solution)/shard_map/all_to_all | solution.py:370
  11.4 10.0 %collective-permute-start = (f32[]{:T(128)}, f32[]{:T(128)}, u32[]{:S(2)}, u32[]{:S(2)}) collective-permute-start(f32[]{:T(128)} %reduce_max.9), channel_id=1, source_target_pairs={{0,8},{8,0},{16,24},{24,16},{1,9},{9,1},{17,25},{25,17},{2,10},{10... | collective-permute-start | bytes 20 | tf_op jit(solution)/shard_map/ppermute | solution.py:167
  15.2 3.2 %copy-start.1 = (f32[1,16,128,128]{3,2,1,0:T(8,128)S(1)}, f32[1,16,128,128]{3,2,1,0:T(8,128)}, u32[]{:S(2)}) copy-start(f32[1,16,128,128]{3,2,1,0:T(8,128)} %param.9) | copy-start | bytes 3145732
  22.6 4.6 %collective-permute-start.1 = (f32[]{:T(128)}, f32[]{:T(128)}, u32[]{:S(2)}, u32[]{:S(2)}) collective-permute-start(f32[]{:T(128)} %max.6), channel_id=1, source_target_pairs={{0,16},{8,24},{16,0},{24,8},{1,17},{9,25},{17,1},{25,9},{2,18},{10... | collective-permute-start | bytes 20 | tf_op jit(solution)/shard_map/ppermute | solution.py:167
  27.9 31.0 %all-to-all-start.1 = ((f32[8,4,128,128]{3,2,1,0:T(8,128)}), f32[8,4,128,128]{3,2,1,0:T(8,128)}, u32[]{:S(2)}, u32[]{:S(2)}) async-start(f32[8,4,128,128]{3,2,1,0:T(8,128)} %bitcast.78), calls=%async_computation.1 | async-start | bytes 4194304 | tf_op jit(solution)/shard_map/all_to_all | solution.py:376
  186.6 18.6 %all-to-all-start.3 = ((f32[8,1,8192]{2,1,0:T(1,128)}), f32[8,1,8192]{2,1,0:T(1,128)S(1)}, u32[]{:S(2)}, u32[]{:S(2)}) async-start(f32[8,1,8192]{2,1,0:T(1,128)} %broadcast_in_dim.5), calls=%async_computation.3 | async-start | bytes 524288 | tf_op jit(solution)/shard_map/all_to_all | solution.py:351

commit v4 on v3

--- a/solution.py
+++ b/solution.py
@@ -131,7 +131,7 @@
 def accumulate(terms, requests, peak, tile_cells):
     slot_count, slice_count = terms.shape[:2]
     patch_side = terms.shape[-1]
-    held = math.gcd(slot_count, 4)
+    held = math.gcd(slot_count, 8)
     grid_spec = pltpu.PrefetchScalarGridSpec(
         num_scalar_prefetch=1,
         grid=(slot_count // held,),
@@ -317,7 +317,7 @@
     side = patches.shape[-1]
     kern = jnp.stack([jnp.cos(prop_phase), jnp.sin(prop_phase)])
     mats_right, mats_left = dft_mats(side)
-    held = math.gcd(count, 4)
+    held = math.gcd(count, 8)
     whole = lambda shape: pl.BlockSpec(shape, lambda k: (0,) * len(shape))
     return pl.pallas_call(
         propagate_kernel,

time: 207 us -> 204 us (0.986)
  no operation moved by 1% of the time
where the time goes in v4:
time: 204 us
  Pallas kernels  129 us (63%)
  starting transfers between devices  18.5 us (9%)
  matrix products  16.1 us (8%)
  other arithmetic  11.5 us (6%)
  blocking collectives  9.35 us (5%)
  local copies, waits for them, and re-layouts  8.51 us (4%)
  waiting for transfers between devices  8.41 us (4%)
  between operations  2.67 us (1%)
    pallas_call x1, Pallas kernels, propagate(): pl.pallas_call(propagate_kernel, grid=(count // held,), in_specs=[pl.Bloc...  115 us
    dot_general x1, matrix products, cut_windows(): jnp.einsum('kscui,kju->kscij', rows, col_sel, preferred_element_type=jnp....  16.1 us
    pallas_call x1, Pallas kernels, accumulate(): pl.pallas_call(place_kernel, grid_spec=grid_spec, out_shape=jax.ShapeDtyp...  13.8 us
    all_to_all x1, blocking collectives, member_sum(): lax.all_to_all(flat, 'member', split_axis=0, concat_axis=0, tiled=True)  9.35 us
    all_to_all x1, waiting for transfers between devices, on_device(): lax.all_to_all(sent.reshape(members, capacity, patch_side, patch_side), '...  7.75 us
    ppermute x2, starting transfers between devices, group_max(): value = jnp.maximum(value, lax.ppermute(value, 'group', pairs))  5.53 us
    all_to_all x1, starting transfers between devices, on_device(): lax.all_to_all(outgoing.reshape(members, capacity, 3), 'member', split_ax...  5.17 us
    all_to_all x1, starting transfers between devices, on_device(): lax.all_to_all(sent.reshape(members, capacity, patch_side, patch_side), '...  4.37 us
  transfers between devices with their start and end apart: 5, of which 2 were waited for; matrix products, arithmetic and copies ran while one was open for 14% of the time, Pallas kernels for 7%

profile of v4, /device:TPU:0, one launch (start us, length us, event | category | flops | bytes accessed | tf_op | source)
XLA Modules:
  0.0 203.6 jit_solution(2524487492591985125)
XLA Ops:
  0.7 0.9 fusion.38
  1.6 0.8 select_reduce_fusion
  2.4 0.7 multiply_add_fusion
  3.2 0.7 concatenate.33
  4.6 5.2 %all-to-all-start = ((s32[8,4,3]{1,2,0:T(4,128)}), s32[8,4,3]{1,2,0:T(4,128)S(1)}, u32[]{:S(2)}, u32[]{:S(2)}) async-start(s32[8,4,3]{1,2,0:T(4,128)} %copy.17), calls=%async_computation | async-start | bytes 32768 | tf_op jit(solution)/shard_map/all_to_all | solution.py:370
  9.8 1.0 multiply_reduce_fusion
  11.4 1.6 collective-permute-start
  14.2 1.0 pad_maximum_fusion.mats_right
  15.2 0.9 pad_maximum_fusion.1.mats_left
  16.8 1.6 broadcast_in_dim.4
  18.4 3.0 %scatter_fusion = f32[32,128,128]{2,1,0:T(8,128)} fusion(f32[32,128,128]{2,1,0:T(8,128)} %broadcast_in_dim.4, s32[16]{0:T(128)S(1)} %fusion.40, f32[16,128,128]{2,1,0:T(8,128)S(1)} %bitcast.80), kind=kCustom, calls=%fused_computation | custom fusion | bytes 3145792 | tf_op jit(solution)/shard_map/scatter | solution.py:373
  22.6 4.0 %collective-permute-start.1 = (f32[]{:T(128)}, f32[]{:T(128)}, u32[]{:S(2)}, u32[]{:S(2)}) collective-permute-start(f32[]{:T(128)} %max.6), channel_id=1, source_target_pairs={{0,16},{8,24},{16,0},{24,8},{1,17},{9,25},{17,1},{25,9},{2,18},{10... | collective-permute-start | bytes 20 | tf_op jit(solution)/shard_map/ppermute | solution.py:167
  27.8 4.4 %all-to-all-start.1 = ((f32[8,4,128,128]{3,2,1,0:T(8,128)}), f32[8,4,128,128]{3,2,1,0:T(8,128)}, u32[]{:S(2)}, u32[]{:S(2)}) async-start(f32[8,4,128,128]{3,2,1,0:T(8,128)} %bitcast.78), calls=%async_computation.1 | async-start | bytes 4194304 | tf_op jit(solution)/shard_map/all_to_all | solution.py:376
  32.4 2.6 %fusion.55 = pred[32,128,512,1,1]{2,1,4,3,0:T(32,128)(4,1)} fusion(s32[32,128]{1,0:T(8,128)S(1)} %get-tuple-element.14), kind=kLoop, calls=%fused_computation.8.clone.clone.clone.clone.2 | loop fusion | flops 2097152 | bytes 2113536 | tf_op jit(solution)/shard_map/kscui,kju->kscij/dot_general | solution.py:65
  35.0 16.1 %fusion.14.patch_ref = bf16[32,2,2,128,128]{4,3,2,1,0:T(8,128)(2,1)} fusion(s32[32,128]{1,0:T(8,128)S(1)} %get-tuple-element.15, bf16[2,2,512,512]{3,2,1,0:T(8,128)(2,1)S(1)} %copy-done, bf16[32]{0:T(256)(128)(2,1)S(1)} %slice_bitcast_fusion.1, pred[32,128,512,1,1]{2,1,4,3,0:T(32,128)(4,1)} %fusion.55), kind=kOutput, calls=%fused_computation.12 | convolution fusion | flops 10752098304 | bytes 8405056 | tf_op jit(solution)/shard_map/kscui,kju->kscij/dot_general | solution.py:65
  51.1 7.7 %all-to-all-done.1 = f32[8,4,128,128]{3,2,1,0:T(8,128)} async-done(((f32[8,4,128,128]{3,2,1,0:T(8,128)}), f32[8,4,128,128]{3,2,1,0:T(8,128)}, u32[]{:S(2)}, u32[]{:S(2)}) %all-to-all-start.1) | async-done | bytes 2097184 | tf_op jit(solution)/shard_map/all_to_all | solution.py:376
  58.9 114.7 %shard_map.77 = (f32[32,2,2,128,128]{4,3,2,1,0:T(8,128)}, f32[2,2,128,128]{3,2,1,0:T(8,128)}) custom-call(bf16[32,2,2,128,128]{4,3,2,1,0:T(8,128)(2,1)} %fusion.14.patch_ref, f32[32,128,128]{2,1,0:T(8,128)} %bitcast.17.measured_ref, f32[2,2,128,128]{3,2,1,0:T(8,128)} %bitcast.79, f32[2,128,128]{2,1,0:T(8,128)} %pad_maximum_fusion.6.kern_ref, ...), custom_call_target="tpu_custom_call" | custom-call | tf_op jit(solution)/shard_map/pallas_call | solution.py:322
  173.6 1.0 broadcast_multiply_fusion
  174.5 9.3 %all_to_all.25 = f32[8,1,8192]{2,1,0:T(1,128)S(1)} all-to-all(f32[8,1,8192]{2,1,0:T(1,128)S(1)} %bitcast.82), channel_id=1, replica_groups=mesh['group'=4,'member'=8] {'member'}, dimensions={0} | all-to-all | bytes 524288 | tf_op jit(solution)/shard_map/all_to_all | solution.py:348
  184.1 0.8 broadcast_in_dim.5
  184.9 3.4 %all-to-all-start.3 = ((f32[8,1,8192]{2,1,0:T(1,128)}), f32[8,1,8192]{2,1,0:T(1,128)S(1)}, u32[]{:S(2)}, u32[]{:S(2)}) async-start(f32[8,1,8192]{2,1,0:T(1,128)} %broadcast_in_dim.5), calls=%async_computation.3 | async-start | bytes 524288 | tf_op jit(solution)/shard_map/all_to_all | solution.py:351
  188.3 0.7 copy.19.requests
  189.0 13.8 %shard_map.78 = f32[2,2,512,512]{3,2,1,0:T(8,128)} custom-call(s32[32,3]{1,0:T(8,128)} %copy.19.requests, f32[1,1]{1,0:T(1,128)} %bitcast.2.peak_ref.peak, f32[32,2,2,128,128]{4,3,2,1,0:T(8,128)} %get-tuple-element.4.terms), custom_call_target="tpu_custom_call" | custom-call | tf_op jit(solution)/shard_map/pallas_call | solution.py:153
  202.8 0.7 copy.27
  (34 shorter events, 4.4 us)
Async XLA Ops:
  0.6 34.4 %copy-start = (bf16[2,2,512,512]{3,2,1,0:T(8,128)(2,1)S(1)}, bf16[2,2,512,512]{3,2,1,0:T(8,128)(2,1)}, u32[]{:S(2)}) copy-start(bf16[2,2,512,512]{3,2,1,0:T(8,128)(2,1)} %param.6) | copy-start | bytes 6291460
  0.6 13.3 %copy-start.3 = (s32[1,16,1]{1,2,0:T(1,128)S(1)}, s32[1,16,1]{1,2,0:T(1,128)}, u32[]{:S(2)}) copy-start(s32[1,16,1]{1,2,0:T(1,128)} %param.10) | copy-start | bytes 196
  0.7 13.3 %copy-start.2 = (f32[128,128]{1,0:T(8,128)S(1)}, f32[128,128]{1,0:T(8,128)}, u32[]{:S(2)}) copy-start(f32[128,128]{1,0:T(8,128)} %param.8) | copy-start | bytes 196612
  4.6 23.2 %all-to-all-start = ((s32[8,4,3]{1,2,0:T(4,128)}), s32[8,4,3]{1,2,0:T(4,128)S(1)}, u32[]{:S(2)}, u32[]{:S(2)}) async-start(s32[8,4,3]{1,2,0:T(4,128)} %copy.17), calls=%async_computation | async-start | bytes 32768 | tf_op jit(solution)/shard_map/all_to_all | solution.py:370
  11.4 9.9 %collective-permute-start = (f32[]{:T(128)}, f32[]{:T(128)}, u32[]{:S(2)}, u32[]{:S(2)}) collective-permute-start(f32[]{:T(128)} %reduce_max.9), channel_id=1, source_target_pairs={{0,8},{8,0},{16,24},{24,16},{1,9},{9,1},{17,25},{25,17},{2,10},{10... | collective-permute-start | bytes 20 | tf_op jit(solution)/shard_map/ppermute | solution.py:167
  15.2 3.2 %copy-start.1 = (f32[1,16,128,128]{3,2,1,0:T(8,128)S(1)}, f32[1,16,128,128]{3,2,1,0:T(8,128)}, u32[]{:S(2)}) copy-start(f32[1,16,128,128]{3,2,1,0:T(8,128)} %param.9) | copy-start | bytes 3145732
  22.6 4.6 %collective-permute-start.1 = (f32[]{:T(128)}, f32[]{:T(128)}, u32[]{:S(2)}, u32[]{:S(2)}) collective-permute-start(f32[]{:T(128)} %max.6), channel_id=1, source_target_pairs={{0,16},{8,24},{16,0},{24,8},{1,17},{9,25},{17,1},{25,9},{2,18},{10... | collective-permute-start | bytes 20 | tf_op jit(solution)/shard_map/ppermute | solution.py:167
  27.8 31.0 %all-to-all-start.1 = ((f32[8,4,128,128]{3,2,1,0:T(8,128)}), f32[8,4,128,128]{3,2,1,0:T(8,128)}, u32[]{:S(2)}, u32[]{:S(2)}) async-start(f32[8,4,128,128]{3,2,1,0:T(8,128)} %bitcast.78), calls=%async_computation.1 | async-start | bytes 4194304 | tf_op jit(solution)/shard_map/all_to_all | solution.py:376
  184.9 17.9 %all-to-all-start.3 = ((f32[8,1,8192]{2,1,0:T(1,128)}), f32[8,1,8192]{2,1,0:T(1,128)S(1)}, u32[]{:S(2)}, u32[]{:S(2)}) async-start(f32[8,1,8192]{2,1,0:T(1,128)} %broadcast_in_dim.5), calls=%async_computation.3 | async-start | bytes 524288 | tf_op jit(solution)/shard_map/all_to_all | solution.py:351

commit v5 on v4

--- a/solution.py
+++ b/solution.py
@@ -362,14 +362,19 @@
     power = jnp.max(jnp.sum(probe_modes * probe_modes, axis=(1, 2)))
     peak_power = group_max(power) + 1e-06
     flat_slots = slot_numbers(tile_owner[0, :, 0], members, capacity)
-    entries = jnp.concatenate([jnp.ones((pos_dev, 1), jnp.int32), corner[0]], axis=1)
-    chosen = (flat_slots[:, None] == jnp.arange(slot_count, dtype=jnp.int32)[None, :]).astype(
-        jnp.int32
-    )
-    outgoing = jnp.sum(chosen[:, :, None] * entries[:, None, :], axis=0)
-    requests = lax.all_to_all(
-        outgoing.reshape(members, capacity, 3), "member", split_axis=0, concat_axis=0, tiled=True
-    ).reshape(slot_count, 3)
+    listed = lax.all_gather(jnp.concatenate([tile_owner[0], corner[0]], axis=1), "member")
+    owners, corners = listed[:, :, 0], listed[:, :, 1:]
+    ranks = jax.vmap(lambda row: slot_numbers(row, members, capacity) - row * capacity)(owners)
+    senders = jnp.arange(members, dtype=jnp.int32)[:, None]
+    mine = (owners == lax.axis_index("member")).reshape(-1)
+    targets = (senders * capacity + ranks).reshape(-1)
+    entries = jnp.concatenate(
+        [jnp.ones((members * pos_dev, 1), jnp.int32), corners.reshape(members * pos_dev, 2)], axis=1
+    )
+    chosen = (
+        (targets[:, None] == jnp.arange(slot_count, dtype=jnp.int32)[None, :]) & mine[:, None]
+    ).astype(jnp.int32)
+    requests = jnp.sum(chosen[:, :, None] * entries[:, None, :], axis=0)
     sent = jnp.zeros((slot_count, patch_side, patch_side), jnp.float32).at[flat_slots].set(
         amplitude[0]
     )

time: 204 us -> 222 us (1.088)
  blocking collectives: 9.35 us -> 39 us
  waiting for transfers between devices: 8.41 us -> 0.53 us
  starting transfers between devices: 18.5 us -> 14.9 us
    all_gather x0 -> x1, blocking collectives: none -> 29.6 us  [on_device(): lax.all_gather(jnp.concatenate([tile_owner[0], corner[0]], axis=1), 'memb...]
    all_to_all x1, waiting for transfers between devices: 7.75 us -> 0.01 us  [on_device(): lax.all_to_all(sent.reshape(members, capacity, patch_side, patch_side), '...]
    all_to_all x1 -> x0, starting transfers between devices: 5.17 us -> none  [on_device(): lax.all_to_all(outgoing.reshape(members, capacity, 3), 'member', split_ax...]
  transfers between devices with their start and end apart: 5 -> 4, of which waited for: 2 -> 1; matrix products, arithmetic and copies ran while one was open for 14% -> 14% of each run, Pallas kernels for 7% -> 6%
where the time goes in v5:
time: 222 us
  Pallas kernels  129 us (58%)
  blocking collectives  39 us (18%)
  matrix products  16.1 us (7%)
  starting transfers between devices  14.9 us (7%)
  other arithmetic  12 us (5%)
  local copies, waits for them, and re-layouts  7.43 us (3%)
  between operations  2.78 us (1%)
    pallas_call x1, Pallas kernels, propagate(): pl.pallas_call(propagate_kernel, grid=(count // held,), in_specs=[pl.Bloc...  115 us
    all_gather x1, blocking collectives, on_device(): lax.all_gather(jnp.concatenate([tile_owner[0], corner[0]], axis=1), 'memb...  29.6 us
    dot_general x1, matrix products, cut_windows(): jnp.einsum('kscui,kju->kscij', rows, col_sel, preferred_element_type=jnp....  16.1 us
    pallas_call x1, Pallas kernels, accumulate(): pl.pallas_call(place_kernel, grid_spec=grid_spec, out_shape=jax.ShapeDtyp...  14 us
    all_to_all x1, blocking collectives, member_sum(): lax.all_to_all(flat, 'member', split_axis=0, concat_axis=0, tiled=True)  9.47 us
    ppermute x2, starting transfers between devices, group_max(): value = jnp.maximum(value, lax.ppermute(value, 'group', pairs))  6.96 us
    all_to_all x1, starting transfers between devices, on_device(): lax.all_to_all(sent.reshape(members, capacity, patch_side, patch_side), '...  4.49 us
  transfers between devices with their start and end apart: 4, of which 1 were waited for; matrix products, arithmetic and copies ran while one was open for 14% of the time, Pallas kernels for 6%

profile of v5, /device:TPU:0, one launch (start us, length us, event | category | flops | bytes accessed | tf_op | source)
XLA Modules:
  0.0 221.6 jit_solution(15443629713804196907)
XLA Ops:
  0.7 1.1 multiply_reduce_fusion
  1.8 0.6 reduce_max.9
  2.4 3.0 %collective-permute-start = (f32[]{:T(128)}, f32[]{:T(128)}, u32[]{:S(2)}, u32[]{:S(2)}) collective-permute-start(f32[]{:T(128)} %reduce_max.9), channel_id=1, source_target_pairs={{0,8},{8,0},{16,24},{24,16},{1,9},{9,1},{17,25},{25,17},{2,10},{10... | collective-permute-start | bytes 20 | tf_op jit(solution)/shard_map/ppermute | solution.py:167
  5.4 0.7 fusion.43
  6.2 0.8 select_reduce_fusion
  7.0 0.7 fusion.44
  7.7 1.5 broadcast_in_dim.4
  9.2 3.0 %scatter_fusion = f32[32,128,128]{2,1,0:T(8,128)} fusion(f32[32,128,128]{2,1,0:T(8,128)} %broadcast_in_dim.4, s32[16]{0:T(128)S(1)} %fusion.44, f32[16,128,128]{2,1,0:T(8,128)S(1)} %bitcast.84), kind=kCustom, calls=%fused_computation | custom fusion | bytes 3145792 | tf_op jit(solution)/shard_map/scatter | solution.py:378
  12.2 4.5 %all-to-all-start = ((f32[8,4,128,128]{3,2,1,0:T(8,128)}), f32[8,4,128,128]{3,2,1,0:T(8,128)}, u32[]{:S(2)}, u32[]{:S(2)}) async-start(f32[8,4,128,128]{3,2,1,0:T(8,128)} %bitcast.82), calls=%async_computation | async-start | bytes 4194304 | tf_op jit(solution)/shard_map/all_to_all | solution.py:381
  16.8 29.6 %all-gather.1 = s32[8,16,3]{1,2,0:T(4,128)S(1)} all-gather(s32[1,16,3]{1,2,0:T(4,128)S(1)} %add_bitcast_fusion), channel_id=2, replica_groups=mesh['group'=4,'member'=8] {'member'}, dimensions={0}, use_global_device_ids=true | all-gather | bytes 1728 | tf_op jit(solution)/shard_map/all_gather | solution.py:365
  48.5 2.6 %fusion.60 = pred[32,128,512,1,1]{2,1,4,3,0:T(32,128)(4,1)} fusion(s32[32,128]{1,0:T(8,128)S(1)} %get-tuple-element.14), kind=kLoop, calls=%fused_computation.8.clone.clone.clone.clone.2 | loop fusion | flops 2097152 | bytes 2113536 | tf_op jit(solution)/shard_map/kscui,kju->kscij/dot_general | solution.py:65
  51.4 1.0 pad_maximum_fusion.mats_right
  52.4 0.9 pad_maximum_fusion.1.mats_left
  53.3 0.6 pad_maximum_fusion.6.kern_ref
  54.0 16.1 %fusion.14.patch_ref = bf16[32,2,2,128,128]{4,3,2,1,0:T(8,128)(2,1)} fusion(s32[32,128]{1,0:T(8,128)S(1)} %get-tuple-element.15, bf16[2,2,512,512]{3,2,1,0:T(8,128)(2,1)S(1)} %copy-done, bf16[32]{0:T(256)(128)(2,1)S(1)} %slice_bitcast_fusion.1, pred[32,128,512,1,1]{2,1,4,3,0:T(32,128)(4,1)} %fusion.60), kind=kOutput, calls=%fused_computation.12 | convolution fusion | flops 10752098304 | bytes 8405056 | tf_op jit(solution)/shard_map/kscui,kju->kscij/dot_general | solution.py:65
  71.3 3.9 %collective-permute-start.1 = (f32[]{:T(128)}, f32[]{:T(128)}, u32[]{:S(2)}, u32[]{:S(2)}) collective-permute-start(f32[]{:T(128)} %max.6), channel_id=1, source_target_pairs={{0,16},{8,24},{16,0},{24,8},{1,17},{9,25},{17,1},{25,9},{2,18},{10... | collective-permute-start | bytes 20 | tf_op jit(solution)/shard_map/ppermute | solution.py:167
  76.5 114.9 %shard_map.77 = (f32[32,2,2,128,128]{4,3,2,1,0:T(8,128)}, f32[2,2,128,128]{3,2,1,0:T(8,128)}) custom-call(bf16[32,2,2,128,128]{4,3,2,1,0:T(8,128)(2,1)} %fusion.14.patch_ref, f32[32,128,128]{2,1,0:T(8,128)} %bitcast.19.measured_ref, f32[2,2,128,128]{3,2,1,0:T(8,128)} %bitcast.83, f32[2,128,128]{2,1,0:T(8,128)} %pad_maximum_fusion.6.kern_ref, ...), custom_call_target="tpu_custom_call" | custom-call | tf_op jit(solution)/shard_map/pallas_call | solution.py:322
  191.4 1.0 broadcast_multiply_fusion
  192.3 9.5 %all_to_all.20 = f32[8,1,8192]{2,1,0:T(1,128)S(1)} all-to-all(f32[8,1,8192]{2,1,0:T(1,128)S(1)} %bitcast.86), channel_id=1, replica_groups=mesh['group'=4,'member'=8] {'member'}, dimensions={0} | all-to-all | bytes 524288 | tf_op jit(solution)/shard_map/all_to_all | solution.py:348
  202.0 0.8 broadcast_in_dim.5
  202.9 3.4 %all-to-all-start.2 = ((f32[8,1,8192]{2,1,0:T(1,128)}), f32[8,1,8192]{2,1,0:T(1,128)S(1)}, u32[]{:S(2)}, u32[]{:S(2)}) async-start(f32[8,1,8192]{2,1,0:T(1,128)} %broadcast_in_dim.5), calls=%async_computation.2 | async-start | bytes 524288 | tf_op jit(solution)/shard_map/all_to_all | solution.py:351
  206.3 0.7 copy.28.requests
  207.0 14.0 %shard_map.78 = f32[2,2,512,512]{3,2,1,0:T(8,128)} custom-call(s32[32,3]{1,0:T(8,128)} %copy.28.requests, f32[1,1]{1,0:T(1,128)} %bitcast.4.peak_ref.peak, f32[32,2,2,128,128]{4,3,2,1,0:T(8,128)} %get-tuple-element.4.terms), custom_call_target="tpu_custom_call" | custom-call | tf_op jit(solution)/shard_map/pallas_call | solution.py:153
  220.9 0.7 copy.37
  (43 shorter events, 3.1 us)
Async XLA Ops:
  0.6 53.3 %copy-start = (bf16[2,2,512,512]{3,2,1,0:T(8,128)(2,1)S(1)}, bf16[2,2,512,512]{3,2,1,0:T(8,128)(2,1)}, u32[]{:S(2)}) copy-start(bf16[2,2,512,512]{3,2,1,0:T(8,128)(2,1)} %param.6) | copy-start | bytes 6291460
  0.6 8.6 %copy-start.1 = (f32[1,16,128,128]{3,2,1,0:T(8,128)S(1)}, f32[1,16,128,128]{3,2,1,0:T(8,128)}, u32[]{:S(2)}) copy-start(f32[1,16,128,128]{3,2,1,0:T(8,128)} %param.9) | copy-start | bytes 3145732
  2.4 67.6 %collective-permute-start = (f32[]{:T(128)}, f32[]{:T(128)}, u32[]{:S(2)}, u32[]{:S(2)}) collective-permute-start(f32[]{:T(128)} %reduce_max.9), channel_id=1, source_target_pairs={{0,8},{8,0},{16,24},{24,16},{1,9},{9,1},{17,25},{25,17},{2,10},{10... | collective-permute-start | bytes 20 | tf_op jit(solution)/shard_map/ppermute | solution.py:167
  12.2 4.5 %copy-start.3 = (s32[1,16,1]{1,2,0:T(1,128)S(1)}, s32[1,16,1]{1,2,0:T(1,128)}, u32[]{:S(2)}) copy-start(s32[1,16,1]{1,2,0:T(1,128)} %param.10) | copy-start | bytes 196
  12.2 4.5 %copy-start.4 = (s32[1,16,2]{1,2,0:T(2,128)S(1)}, s32[1,16,2]{1,2,0:T(2,128)}, u32[]{:S(2)}) copy-start(s32[1,16,2]{1,2,0:T(2,128)} %param.11) | copy-start | bytes 388
  12.2 64.2 %all-to-all-start = ((f32[8,4,128,128]{3,2,1,0:T(8,128)}), f32[8,4,128,128]{3,2,1,0:T(8,128)}, u32[]{:S(2)}, u32[]{:S(2)}) async-start(f32[8,4,128,128]{3,2,1,0:T(8,128)} %bitcast.82), calls=%async_computation | async-start | bytes 4194304 | tf_op jit(solution)/shard_map/all_to_all | solution.py:381
  48.3 2.8 %copy-start.2 = (f32[128,128]{1,0:T(8,128)S(1)}, f32[128,128]{1,0:T(8,128)}, u32[]{:S(2)}) copy-start(f32[128,128]{1,0:T(8,128)} %param.8) | copy-start | bytes 196612
  71.3 4.5 %collective-permute-start.1 = (f32[]{:T(128)}, f32[]{:T(128)}, u32[]{:S(2)}, u32[]{:S(2)}) collective-permute-start(f32[]{:T(128)} %max.6), channel_id=1, source_target_pairs={{0,16},{8,24},{16,0},{24,8},{1,17},{9,25},{17,1},{25,9},{2,18},{10... | collective-permute-start | bytes 20 | tf_op jit(solution)/shard_map/ppermute | solution.py:167
  202.9 18.1 %all-to-all-start.2 = ((f32[8,1,8192]{2,1,0:T(1,128)}), f32[8,1,8192]{2,1,0:T(1,128)S(1)}, u32[]{:S(2)}, u32[]{:S(2)}) async-start(f32[8,1,8192]{2,1,0:T(1,128)} %broadcast_in_dim.5), calls=%async_computation.2 | async-start | bytes 524288 | tf_op jit(solution)/shard_map/all_to_all | solution.py:351

commit v6 on v5

--- a/solution.py
+++ b/solution.py
@@ -375,8 +375,9 @@
         (targets[:, None] == jnp.arange(slot_count, dtype=jnp.int32)[None, :]) & mine[:, None]
     ).astype(jnp.int32)
     requests = jnp.sum(chosen[:, :, None] * entries[:, None, :], axis=0)
+    after_gather = jnp.min(listed).astype(jnp.float32) * 0.0
     sent = jnp.zeros((slot_count, patch_side, patch_side), jnp.float32).at[flat_slots].set(
-        amplitude[0]
+        amplitude[0] + after_gather
     )
     measured = lax.all_to_all(
         sent.reshape(members, capacity, patch_side, patch_side),

time: 222 us -> 206 us (0.928)
  blocking collectives: 39 us -> 19.7 us
  other arithmetic: 12 us -> 14.7 us
    all_gather x1, blocking collectives: 29.6 us -> 8.89 us  [on_device(): lax.all_gather(jnp.concatenate([tile_owner[0], corner[0]], axis=1), 'memb...]
  transfers between devices with their start and end apart: 4 -> 4, of which waited for: 1 -> 1; matrix products, arithmetic and copies ran while one was open for 14% -> 16% of each run, Pallas kernels for 6% -> 7%
where the time goes in v6:
time: 206 us; the launch traced here: 205 us
  Pallas kernels  129 us (63%)
  blocking collectives  19.7 us (10%)
  matrix products  16.1 us (8%)
  other arithmetic  14.7 us (7%)
  starting transfers between devices  14.7 us (7%)
  local copies, waits for them, and re-layouts  7.41 us (4%)
  between operations  3.42 us (2%)
    pallas_call x1, Pallas kernels, propagate(): pl.pallas_call(propagate_kernel, grid=(count // held,), in_specs=[pl.Bloc...  115 us
    dot_general x1, matrix products, cut_windows(): jnp.einsum('kscui,kju->kscij', rows, col_sel, preferred_element_type=jnp....  16.1 us
    pallas_call x1, Pallas kernels, accumulate(): pl.pallas_call(place_kernel, grid_spec=grid_spec, out_shape=jax.ShapeDtyp...  13.8 us
    all_to_all x1, blocking collectives, member_sum(): lax.all_to_all(flat, 'member', split_axis=0, concat_axis=0, tiled=True)  10.8 us
    all_gather x1, blocking collectives, on_device(): lax.all_gather(jnp.concatenate([tile_owner[0], corner[0]], axis=1), 'memb...  8.89 us
    ppermute x2, starting transfers between devices, group_max(): value = jnp.maximum(value, lax.ppermute(value, 'group', pairs))  6.98 us
    all_to_all x1, starting transfers between devices, on_device(): lax.all_to_all(sent.reshape(members, capacity, patch_side, patch_side), '...  4.35 us
  transfers between devices with their start and end apart: 4, of which 1 were waited for; matrix products, arithmetic and copies ran while one was open for 16% of the time, Pallas kernels for 7%

profile of v6, /device:TPU:0, one launch (start us, length us, event | category | flops | bytes accessed | tf_op | source)
XLA Modules:
  0.0 205.2 jit_solution(803470580907885494)
XLA Ops:
  0.6 1.1 multiply_reduce_fusion
  2.4 3.0 %collective-permute-start = (f32[]{:T(128)}, f32[]{:T(128)}, u32[]{:S(2)}, u32[]{:S(2)}) collective-permute-start(f32[]{:T(128)} %reduce_max.9), channel_id=1, source_target_pairs={{0,8},{8,0},{16,24},{24,16},{1,9},{9,1},{17,25},{25,17},{2,10},{10... | collective-permute-start | bytes 20 | tf_op jit(solution)/shard_map/ppermute | solution.py:167
  5.4 0.7 add_bitcast_fusion.1
  6.1 8.9 %all-gather.1 = s32[8,16,3]{1,2,0:T(4,128)S(1)} all-gather(s32[1,16,3]{1,2,0:T(4,128)S(1)} %add_bitcast_fusion.1), channel_id=2, replica_groups=mesh['group'=4,'member'=8] {'member'}, dimensions={0}, use_global_device_ids=true | all-gather | bytes 1728 | tf_op jit(solution)/shard_map/all_gather | solution.py:365
  16.3 0.7 fusion.43
  17.1 0.8 select_reduce_fusion
  17.9 0.7 fusion.44
  18.6 1.3 add_bitcast_fusion
  19.9 1.5 broadcast_in_dim.4
  21.4 3.0 %scatter_fusion = f32[32,128,128]{2,1,0:T(8,128)} fusion(f32[32,128,128]{2,1,0:T(8,128)} %broadcast_in_dim.4, s32[16]{0:T(128)S(1)} %fusion.44, f32[16,128,128]{2,1,0:T(8,128)S(1)} %add_bitcast_fusion), kind=kCustom, calls=%fused_computation | custom fusion | bytes 3145792 | tf_op jit(solution)/shard_map/scatter | solution.py:379
  24.4 4.4 %all-to-all-start = ((f32[8,4,128,128]{3,2,1,0:T(8,128)}), f32[8,4,128,128]{3,2,1,0:T(8,128)}, u32[]{:S(2)}, u32[]{:S(2)}) async-start(f32[8,4,128,128]{3,2,1,0:T(8,128)} %bitcast.83), calls=%async_computation | async-start | bytes 4194304 | tf_op jit(solution)/shard_map/all_to_all | solution.py:382
  30.9 2.6 %fusion.60 = pred[32,128,512,1,1]{2,1,4,3,0:T(32,128)(4,1)} fusion(s32[32,128]{1,0:T(8,128)S(1)} %get-tuple-element.14), kind=kLoop, calls=%fused_computation.8.clone.clone.clone.clone.2 | loop fusion | flops 2097152 | bytes 2113536 | tf_op jit(solution)/shard_map/kscui,kju->kscij/dot_general | solution.py:65
  33.8 1.0 pad_maximum_fusion.mats_right
  34.8 0.9 pad_maximum_fusion.1.mats_left
  36.4 16.1 %fusion.14.patch_ref = bf16[32,2,2,128,128]{4,3,2,1,0:T(8,128)(2,1)} fusion(s32[32,128]{1,0:T(8,128)S(1)} %get-tuple-element.15, bf16[2,2,512,512]{3,2,1,0:T(8,128)(2,1)S(1)} %copy-done, bf16[32]{0:T(256)(128)(2,1)S(1)} %slice_bitcast_fusion.1, pred[32,128,512,1,1]{2,1,4,3,0:T(32,128)(4,1)} %fusion.60), kind=kOutput, calls=%fused_computation.12 | convolution fusion | flops 10752098304 | bytes 8405056 | tf_op jit(solution)/shard_map/kscui,kju->kscij/dot_general | solution.py:65
  53.7 4.0 %collective-permute-start.1 = (f32[]{:T(128)}, f32[]{:T(128)}, u32[]{:S(2)}, u32[]{:S(2)}) collective-permute-start(f32[]{:T(128)} %max.6), channel_id=1, source_target_pairs={{0,16},{8,24},{16,0},{24,8},{1,17},{9,25},{17,1},{25,9},{2,18},{10... | collective-permute-start | bytes 20 | tf_op jit(solution)/shard_map/ppermute | solution.py:167
  58.9 114.9 %shard_map.77 = (f32[32,2,2,128,128]{4,3,2,1,0:T(8,128)}, f32[2,2,128,128]{3,2,1,0:T(8,128)}) custom-call(bf16[32,2,2,128,128]{4,3,2,1,0:T(8,128)(2,1)} %fusion.14.patch_ref, f32[32,128,128]{2,1,0:T(8,128)} %bitcast.19.measured_ref, f32[2,2,128,128]{3,2,1,0:T(8,128)} %bitcast.84, f32[2,128,128]{2,1,0:T(8,128)} %pad_maximum_fusion.6.kern_ref, ...), custom_call_target="tpu_custom_call" | custom-call | tf_op jit(solution)/shard_map/pallas_call | solution.py:322
  173.8 1.0 broadcast_multiply_fusion
  174.8 10.8 %all_to_all.20 = f32[8,1,8192]{2,1,0:T(1,128)S(1)} all-to-all(f32[8,1,8192]{2,1,0:T(1,128)S(1)} %bitcast.86), channel_id=1, replica_groups=mesh['group'=4,'member'=8] {'member'}, dimensions={0} | all-to-all | bytes 524288 | tf_op jit(solution)/shard_map/all_to_all | solution.py:348
  185.8 0.8 broadcast_in_dim.5
  186.6 3.4 %all-to-all-start.2 = ((f32[8,1,8192]{2,1,0:T(1,128)}), f32[8,1,8192]{2,1,0:T(1,128)S(1)}, u32[]{:S(2)}, u32[]{:S(2)}) async-start(f32[8,1,8192]{2,1,0:T(1,128)} %broadcast_in_dim.5), calls=%async_computation.2 | async-start | bytes 524288 | tf_op jit(solution)/shard_map/all_to_all | solution.py:351
  190.0 0.7 copy.28.requests
  190.7 13.8 %shard_map.78 = f32[2,2,512,512]{3,2,1,0:T(8,128)} custom-call(s32[32,3]{1,0:T(8,128)} %copy.28.requests, f32[1,1]{1,0:T(1,128)} %bitcast.4.peak_ref.peak, f32[32,2,2,128,128]{4,3,2,1,0:T(8,128)} %get-tuple-element.4.terms), custom_call_target="tpu_custom_call" | custom-call | tf_op jit(solution)/shard_map/pallas_call | solution.py:153
  204.5 0.7 copy.37
  (39 shorter events, 5.0 us)
Async XLA Ops:
  0.6 35.7 %copy-start = (bf16[2,2,512,512]{3,2,1,0:T(8,128)(2,1)S(1)}, bf16[2,2,512,512]{3,2,1,0:T(8,128)(2,1)}, u32[]{:S(2)}) copy-start(bf16[2,2,512,512]{3,2,1,0:T(8,128)(2,1)} %param.6) | copy-start | bytes 6291460
  2.4 50.1 %collective-permute-start = (f32[]{:T(128)}, f32[]{:T(128)}, u32[]{:S(2)}, u32[]{:S(2)}) collective-permute-start(f32[]{:T(128)} %reduce_max.9), channel_id=1, source_target_pairs={{0,8},{8,0},{16,24},{24,16},{1,9},{9,1},{17,25},{25,17},{2,10},{10... | collective-permute-start | bytes 20 | tf_op jit(solution)/shard_map/ppermute | solution.py:167
  24.4 34.5 %all-to-all-start = ((f32[8,4,128,128]{3,2,1,0:T(8,128)}), f32[8,4,128,128]{3,2,1,0:T(8,128)}, u32[]{:S(2)}, u32[]{:S(2)}) async-start(f32[8,4,128,128]{3,2,1,0:T(8,128)} %bitcast.83), calls=%async_computation | async-start | bytes 4194304 | tf_op jit(solution)/shard_map/all_to_all | solution.py:382
  30.7 2.8 %copy-start.1 = (f32[128,128]{1,0:T(8,128)S(1)}, f32[128,128]{1,0:T(8,128)}, u32[]{:S(2)}) copy-start(f32[128,128]{1,0:T(8,128)} %param.8) | copy-start | bytes 196612
  53.7 4.5 %collective-permute-start.1 = (f32[]{:T(128)}, f32[]{:T(128)}, u32[]{:S(2)}, u32[]{:S(2)}) collective-permute-start(f32[]{:T(128)} %max.6), channel_id=1, source_target_pairs={{0,16},{8,24},{16,0},{24,8},{1,17},{9,25},{17,1},{25,9},{2,18},{10... | collective-permute-start | bytes 20 | tf_op jit(solution)/shard_map/ppermute | solution.py:167
  186.6 17.9 %all-to-all-start.2 = ((f32[8,1,8192]{2,1,0:T(1,128)}), f32[8,1,8192]{2,1,0:T(1,128)S(1)}, u32[]{:S(2)}, u32[]{:S(2)}) async-start(f32[8,1,8192]{2,1,0:T(1,128)} %broadcast_in_dim.5), calls=%async_computation.2 | async-start | bytes 524288 | tf_op jit(solution)/shard_map/all_to_all | solution.py:351

commit v7 on v4

--- a/solution.py
+++ b/solution.py
@@ -191,7 +191,7 @@
     side = fields[0][0].shape[0]
     count = len(fields)
     rows = jnp.concatenate([jnp.concatenate([re, im], axis=1) for re, im in fields], axis=0)
-    mid = jnp.dot(stack_three(rows, 1), right_mat, preferred_element_type=jnp.float32)
+    mid = jnp.dot(rows, right_mat, precision=lax.Precision.HIGH, preferred_element_type=jnp.float32)
     parted = jnp.concatenate(
         [
             jnp.concatenate([mid[m * side:(m + 1) * side, :side] for m in range(count)], axis=1),
@@ -199,7 +199,7 @@
         ],
         axis=0,
     )
-    out = jnp.dot(left_mat, stack_three(parted, 0), preferred_element_type=jnp.float32)
+    out = jnp.dot(left_mat, parted, precision=lax.Precision.HIGH, preferred_element_type=jnp.float32)
     return [
         (out[:side, m * side:(m + 1) * side], out[side:, m * side:(m + 1) * side])
         for m in range(count)
@@ -306,8 +306,8 @@
         high, low = parts(value)
         return jnp.concatenate([high, high, low], axis=1)
 
-    mats_right = jnp.stack([right(minus), right(plus)])
-    mats_left = jnp.stack([left(plus), left(minus)])
+    mats_right = jnp.stack([minus, plus])
+    mats_left = jnp.stack([plus, minus])
     return mats_right, mats_left
 
 
@@ -327,8 +327,8 @@
             pl.BlockSpec((held, side, side), lambda k: (k, 0, 0)),
             whole((modes, 2, side, side)),
             whole((2, side, side)),
-            whole((2, 6 * side, 2 * side)),
-            whole((2, 2 * side, 6 * side)),
+            whole((2, 2 * side, 2 * side)),
+            whole((2, 2 * side, 2 * side)),
             pl.BlockSpec(memory_space=pltpu.SMEM),
         ],
         out_specs=[

time: 204 us -> 205 us (level)
  transfers between devices with their start and end apart: 5 -> 5, of which waited for: 2 -> 2; matrix products, arithmetic and copies ran while one was open for 14% -> 15% of each run, Pallas kernels for 7% -> 7%
where the time goes in v7:
time: 205 us; the launch traced here: 204 us
  Pallas kernels  129 us (63%)
  starting transfers between devices  18.4 us (9%)
  matrix products  16.1 us (8%)
  other arithmetic  11 us (5%)
  local copies, waits for them, and re-layouts  9.37 us (5%)
  blocking collectives  9.35 us (5%)
  waiting for transfers between devices  8.45 us (4%)
  between operations  2.62 us (1%)
    pallas_call x1, Pallas kernels, propagate(): pl.pallas_call(propagate_kernel, grid=(count // held,), in_specs=[pl.Bloc...  115 us
    dot_general x1, matrix products, cut_windows(): jnp.einsum('kscui,kju->kscij', rows, col_sel, preferred_element_type=jnp....  16.1 us
    pallas_call x1, Pallas kernels, accumulate(): pl.pallas_call(place_kernel, grid_spec=grid_spec, out_shape=jax.ShapeDtyp...  13.8 us
    all_to_all x1, blocking collectives, member_sum(): lax.all_to_all(flat, 'member', split_axis=0, concat_axis=0, tiled=True)  9.35 us
    all_to_all x1, waiting for transfers between devices, on_device(): lax.all_to_all(sent.reshape(members, capacity, patch_side, patch_side), '...  7.75 us
    ppermute x2, starting transfers between devices, group_max(): value = jnp.maximum(value, lax.ppermute(value, 'group', pairs))  5.5 us
    all_to_all x1, starting transfers between devices, on_device(): lax.all_to_all(outgoing.reshape(members, capacity, 3), 'member', split_ax...  5.17 us
    all_to_all x1, starting transfers between devices, on_device(): lax.all_to_all(sent.reshape(members, capacity, patch_side, patch_side), '...  4.37 us
  transfers between devices with their start and end apart: 5, of which 2 were waited for; matrix products, arithmetic and copies ran while one was open for 15% of the time, Pallas kernels for 7%

profile of v7, /device:TPU:0, one launch (start us, length us, event | category | flops | bytes accessed | tf_op | source)
XLA Modules:
  0.0 204.2 jit_solution(6359174651330885737)
XLA Ops:
  0.6 0.9 fusion.38
  1.6 0.8 select_reduce_fusion
  3.1 0.7 concatenate.21
  4.6 5.2 %all-to-all-start = ((s32[8,4,3]{1,2,0:T(4,128)}), s32[8,4,3]{1,2,0:T(4,128)S(1)}, u32[]{:S(2)}, u32[]{:S(2)}) async-start(s32[8,4,3]{1,2,0:T(4,128)} %copy.17), calls=%async_computation | async-start | bytes 32768 | tf_op jit(solution)/shard_map/all_to_all | solution.py:370
  9.8 1.0 multiply_reduce_fusion
  11.4 1.6 collective-permute-start
  14.2 1.1 cosine_bitcast_fusion
  15.3 1.1 pad_maximum_fusion.1
  17.0 1.6 broadcast_in_dim.4
  18.6 3.0 %scatter_fusion = f32[32,128,128]{2,1,0:T(8,128)} fusion(f32[32,128,128]{2,1,0:T(8,128)} %broadcast_in_dim.4, s32[16]{0:T(128)S(1)} %fusion.40, f32[16,128,128]{2,1,0:T(8,128)S(1)} %bitcast.76), kind=kCustom, calls=%fused_computation | custom fusion | bytes 3145792 | tf_op jit(solution)/shard_map/scatter | solution.py:373
  22.9 3.9 %collective-permute-start.1 = (f32[]{:T(128)}, f32[]{:T(128)}, u32[]{:S(2)}, u32[]{:S(2)}) collective-permute-start(f32[]{:T(128)} %max.6), channel_id=1, source_target_pairs={{0,16},{8,24},{16,0},{24,8},{1,17},{9,25},{17,1},{25,9},{2,18},{10... | collective-permute-start | bytes 20 | tf_op jit(solution)/shard_map/ppermute | solution.py:167
  26.8 0.7 collective-permute-done.1
  28.1 4.4 %all-to-all-start.1 = ((f32[8,4,128,128]{3,2,1,0:T(8,128)}), f32[8,4,128,128]{3,2,1,0:T(8,128)}, u32[]{:S(2)}, u32[]{:S(2)}) async-start(f32[8,4,128,128]{3,2,1,0:T(8,128)} %bitcast.74), calls=%async_computation.1 | async-start | bytes 4194304 | tf_op jit(solution)/shard_map/all_to_all | solution.py:376
  32.7 2.6 %fusion.55 = pred[32,128,512,1,1]{2,1,4,3,0:T(32,128)(4,1)} fusion(s32[32,128]{1,0:T(8,128)S(1)} %get-tuple-element.14), kind=kLoop, calls=%fused_computation.8.clone.clone.clone.clone.2 | loop fusion | flops 2097152 | bytes 2113536 | tf_op jit(solution)/shard_map/kscui,kju->kscij/dot_general | solution.py:65
  35.3 16.1 %fusion.14.patch_ref = bf16[32,2,2,128,128]{4,3,2,1,0:T(8,128)(2,1)} fusion(s32[32,128]{1,0:T(8,128)S(1)} %get-tuple-element.15, bf16[2,2,512,512]{3,2,1,0:T(8,128)(2,1)S(1)} %copy-done, bf16[32]{0:T(256)(128)(2,1)S(1)} %slice_bitcast_fusion.1, pred[32,128,512,1,1]{2,1,4,3,0:T(32,128)(4,1)} %fusion.55), kind=kOutput, calls=%fused_computation.12 | convolution fusion | flops 10752098304 | bytes 8405056 | tf_op jit(solution)/shard_map/kscui,kju->kscij/dot_general | solution.py:65
  51.4 7.8 %all-to-all-done.1 = f32[8,4,128,128]{3,2,1,0:T(8,128)} async-done(((f32[8,4,128,128]{3,2,1,0:T(8,128)}), f32[8,4,128,128]{3,2,1,0:T(8,128)}, u32[]{:S(2)}, u32[]{:S(2)}) %all-to-all-start.1) | async-done | bytes 2097184 | tf_op jit(solution)/shard_map/all_to_all | solution.py:376
  59.1 115.1 %shard_map.77 = (f32[32,2,2,128,128]{4,3,2,1,0:T(8,128)}, f32[2,2,128,128]{3,2,1,0:T(8,128)}) custom-call(bf16[32,2,2,128,128]{4,3,2,1,0:T(8,128)(2,1)} %fusion.14.patch_ref, f32[32,128,128]{2,1,0:T(8,128)} %bitcast.17.measured_ref, f32[2,2,128,128]{3,2,1,0:T(8,128)} %bitcast.75, f32[2,128,128]{2,1,0:T(8,128)} %pad_maximum_fusion.6.kern_ref, ...), custom_call_target="tpu_custom_call" | custom-call | tf_op jit(solution)/shard_map/pallas_call | solution.py:322
  174.2 1.0 broadcast_multiply_fusion
  175.2 9.3 %all_to_all.25 = f32[8,1,8192]{2,1,0:T(1,128)S(1)} all-to-all(f32[8,1,8192]{2,1,0:T(1,128)S(1)} %bitcast.78), channel_id=1, replica_groups=mesh['group'=4,'member'=8] {'member'}, dimensions={0} | all-to-all | bytes 524288 | tf_op jit(solution)/shard_map/all_to_all | solution.py:348
  184.8 0.8 broadcast_in_dim.5
  185.6 3.4 %all-to-all-start.3 = ((f32[8,1,8192]{2,1,0:T(1,128)}), f32[8,1,8192]{2,1,0:T(1,128)S(1)}, u32[]{:S(2)}, u32[]{:S(2)}) async-start(f32[8,1,8192]{2,1,0:T(1,128)} %broadcast_in_dim.5), calls=%async_computation.3 | async-start | bytes 524288 | tf_op jit(solution)/shard_map/all_to_all | solution.py:351
  189.0 0.7 copy.19.requests
  189.7 13.8 %shard_map.78 = f32[2,2,512,512]{3,2,1,0:T(8,128)} custom-call(s32[32,3]{1,0:T(8,128)} %copy.19.requests, f32[1,1]{1,0:T(1,128)} %bitcast.2.peak_ref.peak, f32[32,2,2,128,128]{4,3,2,1,0:T(8,128)} %get-tuple-element.4.terms), custom_call_target="tpu_custom_call" | custom-call | tf_op jit(solution)/shard_map/pallas_call | solution.py:153
  203.5 0.7 copy.27
  (26 shorter events, 4.5 us)
Async XLA Ops:
  0.6 34.7 %copy-start = (bf16[2,2,512,512]{3,2,1,0:T(8,128)(2,1)S(1)}, bf16[2,2,512,512]{3,2,1,0:T(8,128)(2,1)}, u32[]{:S(2)}) copy-start(bf16[2,2,512,512]{3,2,1,0:T(8,128)(2,1)} %param.6) | copy-start | bytes 6291460
  4.6 23.5 %all-to-all-start = ((s32[8,4,3]{1,2,0:T(4,128)}), s32[8,4,3]{1,2,0:T(4,128)S(1)}, u32[]{:S(2)}, u32[]{:S(2)}) async-start(s32[8,4,3]{1,2,0:T(4,128)} %copy.17), calls=%async_computation | async-start | bytes 32768 | tf_op jit(solution)/shard_map/all_to_all | solution.py:370
  11.4 10.2 %collective-permute-start = (f32[]{:T(128)}, f32[]{:T(128)}, u32[]{:S(2)}, u32[]{:S(2)}) collective-permute-start(f32[]{:T(128)} %reduce_max.9), channel_id=1, source_target_pairs={{0,8},{8,0},{16,24},{24,16},{1,9},{9,1},{17,25},{25,17},{2,10},{10... | collective-permute-start | bytes 20 | tf_op jit(solution)/shard_map/ppermute | solution.py:167
  15.3 3.3 %copy-start.1 = (f32[1,16,128,128]{3,2,1,0:T(8,128)S(1)}, f32[1,16,128,128]{3,2,1,0:T(8,128)}, u32[]{:S(2)}) copy-start(f32[1,16,128,128]{3,2,1,0:T(8,128)} %param.9) | copy-start | bytes 3145732
  22.9 4.6 %collective-permute-start.1 = (f32[]{:T(128)}, f32[]{:T(128)}, u32[]{:S(2)}, u32[]{:S(2)}) collective-permute-start(f32[]{:T(128)} %max.6), channel_id=1, source_target_pairs={{0,16},{8,24},{16,0},{24,8},{1,17},{9,25},{17,1},{25,9},{2,18},{10... | collective-permute-start | bytes 20 | tf_op jit(solution)/shard_map/ppermute | solution.py:167
  28.1 31.0 %all-to-all-start.1 = ((f32[8,4,128,128]{3,2,1,0:T(8,128)}), f32[8,4,128,128]{3,2,1,0:T(8,128)}, u32[]{:S(2)}, u32[]{:S(2)}) async-start(f32[8,4,128,128]{3,2,1,0:T(8,128)} %bitcast.74), calls=%async_computation.1 | async-start | bytes 4194304 | tf_op jit(solution)/shard_map/all_to_all | solution.py:376
  185.6 17.9 %all-to-all-start.3 = ((f32[8,1,8192]{2,1,0:T(1,128)}), f32[8,1,8192]{2,1,0:T(1,128)S(1)}, u32[]{:S(2)}, u32[]{:S(2)}) async-start(f32[8,1,8192]{2,1,0:T(1,128)} %broadcast_in_dim.5), calls=%async_computation.3 | async-start | bytes 524288 | tf_op jit(solution)/shard_map/all_to_all | solution.py:351

commit v8 on v4

--- a/solution.py
+++ b/solution.py
@@ -212,29 +212,38 @@
     def _():
         probe_sum_ref[...] = jnp.zeros_like(probe_sum_ref)
 
-    for held in range(patch_ref.shape[0]):
-        propagate_one(held, patch_ref, measured_ref, probe_ref, kern_ref, mats_right, mats_left,
-                      grad_ref, probe_sum_ref)
-
-
-def propagate_one(held, patch_ref, measured_ref, probe_ref, kern_ref, mats_right, mats_left,
-                  grad_ref, probe_sum_ref):
+    held = patch_ref.shape[0]
+    together = 2 if held % 2 == 0 else 1
+    for first in range(0, held, together):
+        propagate_group(list(range(first, first + together)), patch_ref, measured_ref, probe_ref,
+                        kern_ref, mats_right, mats_left, grad_ref, probe_sum_ref)
+
+
+def propagate_group(slots, patch_ref, measured_ref, probe_ref, kern_ref, mats_right, mats_left,
+                    grad_ref, probe_sum_ref):
     slice_count = patch_ref.shape[1]
     modes = probe_ref.shape[0]
     forward = lambda fields: fourier_2d(fields, mats_right[0], mats_left[0])
     inverse = lambda fields: fourier_2d(fields, mats_right[1], mats_left[1])
     kern_real, kern_imag = kern_ref[0], kern_ref[1]
-    waves = [(probe_ref[m, 0], probe_ref[m, 1]) for m in range(modes)]
+    owner = [j for j in range(len(slots)) for _ in range(modes)]
+    waves = [(probe_ref[m, 0], probe_ref[m, 1]) for _ in slots for m in range(modes)]
+
+    def patch(layer):
+        return [
+            (patch_ref[s, layer, 0].astype(jnp.float32), patch_ref[s, layer, 1].astype(jnp.float32))
+            for s in slots
+        ]
+
     history = []
     leaving = None
     for layer in range(slice_count):
         history.append(waves)
-        patch_real = patch_ref[held, layer, 0].astype(jnp.float32)
-        patch_imag = patch_ref[held, layer, 1].astype(jnp.float32)
-        leaving = [
-            (wr * patch_real - wi * patch_imag, wr * patch_imag + wi * patch_real)
-            for wr, wi in waves
-        ]
+        cells = patch(layer)
+        leaving = []
+        for (wr, wi), j in zip(waves, owner):
+            pr, pi = cells[j]
+            leaving.append((wr * pr - wi * pi, wr * pi + wi * pr))
         if layer < slice_count - 1:
             spectra = forward(leaving)
             waves = inverse(
@@ -244,28 +253,37 @@
                 ]
             )
     far = forward(leaving)
-    intensity = None
-    for fr, fi in far:
-        power = fr * fr + fi * fi
-        intensity = power if intensity is None else intensity + power
-    factor = 1.0 - measured_ref[held] / jnp.sqrt(jnp.maximum(intensity, 1.0))
-    back = inverse([(fr * factor, fi * factor) for fr, fi in far])
+    scaled = []
+    for j, s in enumerate(slots):
+        intensity = None
+        for m in range(modes):
+            fr, fi = far[j * modes + m]
+            power = fr * fr + fi * fi
+            intensity = power if intensity is None else intensity + power
+        factor = 1.0 - measured_ref[s] / jnp.sqrt(jnp.maximum(intensity, 1.0))
+        for m in range(modes):
+            fr, fi = far[j * modes + m]
+            scaled.append((fr * factor, fi * factor))
+    back = inverse(scaled)
     for layer in reversed(range(slice_count)):
-        grad_real = None
-        grad_imag = None
-        for (wr, wi), (br, bi) in zip(history[layer], back):
-            term_real = wr * br + wi * bi
-            term_imag = wr * bi - wi * br
-            grad_real = term_real if grad_real is None else grad_real + term_real
-            grad_imag = term_imag if grad_imag is None else grad_imag + term_imag
-        grad_ref[held, layer, 0] = grad_real
-        grad_ref[held, layer, 1] = grad_imag
-        patch_real = patch_ref[held, layer, 0].astype(jnp.float32)
-        patch_imag = patch_ref[held, layer, 1].astype(jnp.float32)
-        back = [
-            (patch_real * br + patch_imag * bi, patch_real * bi - patch_imag * br)
-            for br, bi in back
-        ]
+        for j, s in enumerate(slots):
+            grad_real = None
+            grad_imag = None
+            for m in range(modes):
+                wr, wi = history[layer][j * modes + m]
+                br, bi = back[j * modes + m]
+                term_real = wr * br + wi * bi
+                term_imag = wr * bi - wi * br
+                grad_real = term_real if grad_real is None else grad_real + term_real
+                grad_imag = term_imag if grad_imag is None else grad_imag + term_imag
+            grad_ref[s, layer, 0] = grad_real
+            grad_ref[s, layer, 1] = grad_imag
+        cells = patch(layer)
+        moved = []
+        for (br, bi), j in zip(back, owner):
+            pr, pi = cells[j]
+            moved.append((pr * br + pi * bi, pr * bi - pi * br))
+        back = moved
         if layer > 0:
             spectra = forward(back)
             back = inverse(
@@ -274,10 +292,11 @@
                     for fr, fi in spectra
                 ]
             )
-
-    for mode, (br, bi) in enumerate(back):
-        probe_sum_ref[mode, 0] = probe_sum_ref[mode, 0] + br
-        probe_sum_ref[mode, 1] = probe_sum_ref[mode, 1] + bi
+    for j in range(len(slots)):
+        for m in range(modes):
+            br, bi = back[j * modes + m]
+            probe_sum_ref[m, 0] = probe_sum_ref[m, 0] + br
+            probe_sum_ref[m, 1] = probe_sum_ref[m, 1] + bi
 
 
 def dft_mats(length):

time: 204 us -> 177 us (0.87)
  Pallas kernels: 129 us -> 101 us
    pallas_call x1, Pallas kernels: 115 us -> 87.1 us  [propagate(): pl.pallas_call(propagate_kernel, grid=(count // held,), in_specs=[pl.Bloc...]
  transfers between devices with their start and end apart: 5 -> 5, of which waited for: 2 -> 2; matrix products, arithmetic and copies ran while one was open for 14% -> 17% of each run, Pallas kernels for 7% -> 8%
where the time goes in v8:
time: 177 us; the launch traced here: 176 us
  Pallas kernels  101 us (57%)
  starting transfers between devices  18.5 us (10%)
  matrix products  16.1 us (9%)
  other arithmetic  11.5 us (6%)
  blocking collectives  9.35 us (5%)
  local copies, waits for them, and re-layouts  8.52 us (5%)
  waiting for transfers between devices  8.42 us (5%)
  between operations  2.67 us (2%)
    pallas_call x1, Pallas kernels, propagate(): pl.pallas_call(propagate_kernel, grid=(count // held,), in_specs=[pl.Bloc...  87.1 us
    dot_general x1, matrix products, cut_windows(): jnp.einsum('kscui,kju->kscij', rows, col_sel, preferred_element_type=jnp....  16.1 us
    pallas_call x1, Pallas kernels, accumulate(): pl.pallas_call(place_kernel, grid_spec=grid_spec, out_shape=jax.ShapeDtyp...  14 us
    all_to_all x1, blocking collectives, member_sum(): lax.all_to_all(flat, 'member', split_axis=0, concat_axis=0, tiled=True)  9.35 us
    all_to_all x1, waiting for transfers between devices, on_device(): lax.all_to_all(sent.reshape(members, capacity, patch_side, patch_side), '...  7.75 us
    ppermute x2, starting transfers between devices, group_max(): value = jnp.maximum(value, lax.ppermute(value, 'group', pairs))  5.53 us
    all_to_all x1, starting transfers between devices, on_device(): lax.all_to_all(outgoing.reshape(members, capacity, 3), 'member', split_ax...  5.17 us
    all_to_all x1, starting transfers between devices, on_device(): lax.all_to_all(sent.reshape(members, capacity, patch_side, patch_side), '...  4.37 us
  transfers between devices with their start and end apart: 5, of which 2 were waited for; matrix products, arithmetic and copies ran while one was open for 17% of the time, Pallas kernels for 8%

profile of v8, /device:TPU:0, one launch (start us, length us, event | category | flops | bytes accessed | tf_op | source)
XLA Modules:
  0.0 176.1 jit_solution(7895305970083045103)
XLA Ops:
  0.7 0.9 fusion.38
  1.6 0.8 select_reduce_fusion
  2.4 0.7 multiply_add_fusion
  3.2 0.7 concatenate.33
  4.6 5.2 %all-to-all-start = ((s32[8,4,3]{1,2,0:T(4,128)}), s32[8,4,3]{1,2,0:T(4,128)S(1)}, u32[]{:S(2)}, u32[]{:S(2)}) async-start(s32[8,4,3]{1,2,0:T(4,128)} %copy.17), calls=%async_computation | async-start | bytes 32768 | tf_op jit(solution)/shard_map/all_to_all | solution.py:389
  9.8 1.0 multiply_reduce_fusion
  11.4 1.6 collective-permute-start
  14.2 1.0 pad_maximum_fusion.mats_right
  15.2 0.9 pad_maximum_fusion.1.mats_left
  16.8 1.6 broadcast_in_dim.4
  18.4 3.0 %scatter_fusion = f32[32,128,128]{2,1,0:T(8,128)} fusion(f32[32,128,128]{2,1,0:T(8,128)} %broadcast_in_dim.4, s32[16]{0:T(128)S(1)} %fusion.40, f32[16,128,128]{2,1,0:T(8,128)S(1)} %bitcast.80), kind=kCustom, calls=%fused_computation | custom fusion | bytes 3145792 | tf_op jit(solution)/shard_map/scatter | solution.py:392
  22.6 3.9 %collective-permute-start.1 = (f32[]{:T(128)}, f32[]{:T(128)}, u32[]{:S(2)}, u32[]{:S(2)}) collective-permute-start(f32[]{:T(128)} %max.6), channel_id=1, source_target_pairs={{0,16},{8,24},{16,0},{24,8},{1,17},{9,25},{17,1},{25,9},{2,18},{10... | collective-permute-start | bytes 20 | tf_op jit(solution)/shard_map/ppermute | solution.py:167
  27.8 4.4 %all-to-all-start.1 = ((f32[8,4,128,128]{3,2,1,0:T(8,128)}), f32[8,4,128,128]{3,2,1,0:T(8,128)}, u32[]{:S(2)}, u32[]{:S(2)}) async-start(f32[8,4,128,128]{3,2,1,0:T(8,128)} %bitcast.78), calls=%async_computation.1 | async-start | bytes 4194304 | tf_op jit(solution)/shard_map/all_to_all | solution.py:395
  32.4 2.6 %fusion.55 = pred[32,128,512,1,1]{2,1,4,3,0:T(32,128)(4,1)} fusion(s32[32,128]{1,0:T(8,128)S(1)} %get-tuple-element.14), kind=kLoop, calls=%fused_computation.8.clone.clone.clone.clone.2 | loop fusion | flops 2097152 | bytes 2113536 | tf_op jit(solution)/shard_map/kscui,kju->kscij/dot_general | solution.py:65
  35.0 16.1 %fusion.14.patch_ref = bf16[32,2,2,128,128]{4,3,2,1,0:T(8,128)(2,1)} fusion(s32[32,128]{1,0:T(8,128)S(1)} %get-tuple-element.15, bf16[2,2,512,512]{3,2,1,0:T(8,128)(2,1)S(1)} %copy-done, bf16[32]{0:T(256)(128)(2,1)S(1)} %slice_bitcast_fusion.1, pred[32,128,512,1,1]{2,1,4,3,0:T(32,128)(4,1)} %fusion.55), kind=kOutput, calls=%fused_computation.12 | convolution fusion | flops 10752098304 | bytes 8405056 | tf_op jit(solution)/shard_map/kscui,kju->kscij/dot_general | solution.py:65
  51.1 7.8 %all-to-all-done.1 = f32[8,4,128,128]{3,2,1,0:T(8,128)} async-done(((f32[8,4,128,128]{3,2,1,0:T(8,128)}), f32[8,4,128,128]{3,2,1,0:T(8,128)}, u32[]{:S(2)}, u32[]{:S(2)}) %all-to-all-start.1) | async-done | bytes 2097184 | tf_op jit(solution)/shard_map/all_to_all | solution.py:395
  58.9 87.1 %shard_map.77 = (f32[32,2,2,128,128]{4,3,2,1,0:T(8,128)}, f32[2,2,128,128]{3,2,1,0:T(8,128)}) custom-call(bf16[32,2,2,128,128]{4,3,2,1,0:T(8,128)(2,1)} %fusion.14.patch_ref, f32[32,128,128]{2,1,0:T(8,128)} %bitcast.17.measured_ref, f32[2,2,128,128]{3,2,1,0:T(8,128)} %bitcast.79, f32[2,128,128]{2,1,0:T(8,128)} %pad_maximum_fusion.6.kern_ref, ...), custom_call_target="tpu_custom_call" | custom-call | tf_op jit(solution)/shard_map/pallas_call | solution.py:341
  146.0 1.0 broadcast_multiply_fusion
  146.9 9.3 %all_to_all.25 = f32[8,1,8192]{2,1,0:T(1,128)S(1)} all-to-all(f32[8,1,8192]{2,1,0:T(1,128)S(1)} %bitcast.82), channel_id=1, replica_groups=mesh['group'=4,'member'=8] {'member'}, dimensions={0} | all-to-all | bytes 524288 | tf_op jit(solution)/shard_map/all_to_all | solution.py:367
  156.5 0.8 broadcast_in_dim.5
  157.3 3.4 %all-to-all-start.3 = ((f32[8,1,8192]{2,1,0:T(1,128)}), f32[8,1,8192]{2,1,0:T(1,128)S(1)}, u32[]{:S(2)}, u32[]{:S(2)}) async-start(f32[8,1,8192]{2,1,0:T(1,128)} %broadcast_in_dim.5), calls=%async_computation.3 | async-start | bytes 524288 | tf_op jit(solution)/shard_map/all_to_all | solution.py:370
  160.8 0.7 copy.19.requests
  161.4 14.0 %shard_map.78 = f32[2,2,512,512]{3,2,1,0:T(8,128)} custom-call(s32[32,3]{1,0:T(8,128)} %copy.19.requests, f32[1,1]{1,0:T(1,128)} %bitcast.2.peak_ref.peak, f32[32,2,2,128,128]{4,3,2,1,0:T(8,128)} %get-tuple-element.4.terms), custom_call_target="tpu_custom_call" | custom-call | tf_op jit(solution)/shard_map/pallas_call | solution.py:153
  175.4 0.7 copy.27
  (34 shorter events, 4.4 us)
Async XLA Ops:
  0.6 34.4 %copy-start = (bf16[2,2,512,512]{3,2,1,0:T(8,128)(2,1)S(1)}, bf16[2,2,512,512]{3,2,1,0:T(8,128)(2,1)}, u32[]{:S(2)}) copy-start(bf16[2,2,512,512]{3,2,1,0:T(8,128)(2,1)} %param.6) | copy-start | bytes 6291460
  0.6 13.3 %copy-start.3 = (s32[1,16,1]{1,2,0:T(1,128)S(1)}, s32[1,16,1]{1,2,0:T(1,128)}, u32[]{:S(2)}) copy-start(s32[1,16,1]{1,2,0:T(1,128)} %param.10) | copy-start | bytes 196
  0.7 13.3 %copy-start.2 = (f32[128,128]{1,0:T(8,128)S(1)}, f32[128,128]{1,0:T(8,128)}, u32[]{:S(2)}) copy-start(f32[128,128]{1,0:T(8,128)} %param.8) | copy-start | bytes 196612
  4.6 23.2 %all-to-all-start = ((s32[8,4,3]{1,2,0:T(4,128)}), s32[8,4,3]{1,2,0:T(4,128)S(1)}, u32[]{:S(2)}, u32[]{:S(2)}) async-start(s32[8,4,3]{1,2,0:T(4,128)} %copy.17), calls=%async_computation | async-start | bytes 32768 | tf_op jit(solution)/shard_map/all_to_all | solution.py:389
  11.4 9.9 %collective-permute-start = (f32[]{:T(128)}, f32[]{:T(128)}, u32[]{:S(2)}, u32[]{:S(2)}) collective-permute-start(f32[]{:T(128)} %reduce_max.9), channel_id=1, source_target_pairs={{0,8},{8,0},{16,24},{24,16},{1,9},{9,1},{17,25},{25,17},{2,10},{10... | collective-permute-start | bytes 20 | tf_op jit(solution)/shard_map/ppermute | solution.py:167
  15.2 3.2 %copy-start.1 = (f32[1,16,128,128]{3,2,1,0:T(8,128)S(1)}, f32[1,16,128,128]{3,2,1,0:T(8,128)}, u32[]{:S(2)}) copy-start(f32[1,16,128,128]{3,2,1,0:T(8,128)} %param.9) | copy-start | bytes 3145732
  22.6 4.6 %collective-permute-start.1 = (f32[]{:T(128)}, f32[]{:T(128)}, u32[]{:S(2)}, u32[]{:S(2)}) collective-permute-start(f32[]{:T(128)} %max.6), channel_id=1, source_target_pairs={{0,16},{8,24},{16,0},{24,8},{1,17},{9,25},{17,1},{25,9},{2,18},{10... | collective-permute-start | bytes 20 | tf_op jit(solution)/shard_map/ppermute | solution.py:167
  27.8 31.0 %all-to-all-start.1 = ((f32[8,4,128,128]{3,2,1,0:T(8,128)}), f32[8,4,128,128]{3,2,1,0:T(8,128)}, u32[]{:S(2)}, u32[]{:S(2)}) async-start(f32[8,4,128,128]{3,2,1,0:T(8,128)} %bitcast.78), calls=%async_computation.1 | async-start | bytes 4194304 | tf_op jit(solution)/shard_map/all_to_all | solution.py:395
  157.3 18.1 %all-to-all-start.3 = ((f32[8,1,8192]{2,1,0:T(1,128)}), f32[8,1,8192]{2,1,0:T(1,128)S(1)}, u32[]{:S(2)}, u32[]{:S(2)}) async-start(f32[8,1,8192]{2,1,0:T(1,128)} %broadcast_in_dim.5), calls=%async_computation.3 | async-start | bytes 524288 | tf_op jit(solution)/shard_map/all_to_all | solution.py:370

commit v9 on v8

--- a/solution.py
+++ b/solution.py
@@ -213,7 +213,7 @@
         probe_sum_ref[...] = jnp.zeros_like(probe_sum_ref)
 
     held = patch_ref.shape[0]
-    together = 2 if held % 2 == 0 else 1
+    together = math.gcd(held, 4)
     for first in range(0, held, together):
         propagate_group(list(range(first, first + together)), patch_ref, measured_ref, probe_ref,
                         kern_ref, mats_right, mats_left, grad_ref, probe_sum_ref)

time: 177 us -> 164 us (0.927)
  Pallas kernels: 101 us -> 88.4 us
    pallas_call x1, Pallas kernels: 87.1 us -> 74.6 us  [propagate(): pl.pallas_call(propagate_kernel, grid=(count // held,), in_specs=[pl.Bloc...]
  transfers between devices with their start and end apart: 5 -> 5, of which waited for: 2 -> 2; matrix products, arithmetic and copies ran while one was open for 17% -> 18% of each run, Pallas kernels for 8% -> 8%
where the time goes in v9:
time: 164 us; the launch traced here: 163 us
  Pallas kernels  88.4 us (54%)
  starting transfers between devices  18.5 us (11%)
  matrix products  16.1 us (10%)
  other arithmetic  11.5 us (7%)
  blocking collectives  9.35 us (6%)
  local copies, waits for them, and re-layouts  8.52 us (5%)
  waiting for transfers between devices  8.41 us (5%)
  between operations  2.67 us (2%)
    pallas_call x1, Pallas kernels, propagate(): pl.pallas_call(propagate_kernel, grid=(count // held,), in_specs=[pl.Bloc...  74.6 us
    dot_general x1, matrix products, cut_windows(): jnp.einsum('kscui,kju->kscij', rows, col_sel, preferred_element_type=jnp....  16.1 us
    pallas_call x1, Pallas kernels, accumulate(): pl.pallas_call(place_kernel, grid_spec=grid_spec, out_shape=jax.ShapeDtyp...  13.8 us
    all_to_all x1, blocking collectives, member_sum(): lax.all_to_all(flat, 'member', split_axis=0, concat_axis=0, tiled=True)  9.35 us
    all_to_all x1, waiting for transfers between devices, on_device(): lax.all_to_all(sent.reshape(members, capacity, patch_side, patch_side), '...  7.75 us
    ppermute x2, starting transfers between devices, group_max(): value = jnp.maximum(value, lax.ppermute(value, 'group', pairs))  5.53 us
    all_to_all x1, starting transfers between devices, on_device(): lax.all_to_all(outgoing.reshape(members, capacity, 3), 'member', split_ax...  5.17 us
    all_to_all x1, starting transfers between devices, on_device(): lax.all_to_all(sent.reshape(members, capacity, patch_side, patch_side), '...  4.37 us
  transfers between devices with their start and end apart: 5, of which 2 were waited for; matrix products, arithmetic and copies ran while one was open for 18% of the time, Pallas kernels for 8%

profile of v9, /device:TPU:0, one launch (start us, length us, event | category | flops | bytes accessed | tf_op | source)
XLA Modules:
  0.0 163.4 jit_solution(5197088180991239825)
XLA Ops:
  0.7 0.9 fusion.38
  1.6 0.8 select_reduce_fusion
  2.4 0.7 multiply_add_fusion
  3.2 0.7 concatenate.33
  4.6 5.2 %all-to-all-start = ((s32[8,4,3]{1,2,0:T(4,128)}), s32[8,4,3]{1,2,0:T(4,128)S(1)}, u32[]{:S(2)}, u32[]{:S(2)}) async-start(s32[8,4,3]{1,2,0:T(4,128)} %copy.17), calls=%async_computation | async-start | bytes 32768 | tf_op jit(solution)/shard_map/all_to_all | solution.py:389
  9.8 1.0 multiply_reduce_fusion
  11.4 1.6 collective-permute-start
  14.2 1.0 pad_maximum_fusion.mats_right
  15.2 0.9 pad_maximum_fusion.1.mats_left
  16.8 1.6 broadcast_in_dim.4
  18.4 3.0 %scatter_fusion = f32[32,128,128]{2,1,0:T(8,128)} fusion(f32[32,128,128]{2,1,0:T(8,128)} %broadcast_in_dim.4, s32[16]{0:T(128)S(1)} %fusion.40, f32[16,128,128]{2,1,0:T(8,128)S(1)} %bitcast.80), kind=kCustom, calls=%fused_computation | custom fusion | bytes 3145792 | tf_op jit(solution)/shard_map/scatter | solution.py:392
  22.6 4.0 %collective-permute-start.1 = (f32[]{:T(128)}, f32[]{:T(128)}, u32[]{:S(2)}, u32[]{:S(2)}) collective-permute-start(f32[]{:T(128)} %max.6), channel_id=1, source_target_pairs={{0,16},{8,24},{16,0},{24,8},{1,17},{9,25},{17,1},{25,9},{2,18},{10... | collective-permute-start | bytes 20 | tf_op jit(solution)/shard_map/ppermute | solution.py:167
  27.9 4.4 %all-to-all-start.1 = ((f32[8,4,128,128]{3,2,1,0:T(8,128)}), f32[8,4,128,128]{3,2,1,0:T(8,128)}, u32[]{:S(2)}, u32[]{:S(2)}) async-start(f32[8,4,128,128]{3,2,1,0:T(8,128)} %bitcast.78), calls=%async_computation.1 | async-start | bytes 4194304 | tf_op jit(solution)/shard_map/all_to_all | solution.py:395
  32.4 2.6 %fusion.55 = pred[32,128,512,1,1]{2,1,4,3,0:T(32,128)(4,1)} fusion(s32[32,128]{1,0:T(8,128)S(1)} %get-tuple-element.14), kind=kLoop, calls=%fused_computation.8.clone.clone.clone.clone.2 | loop fusion | flops 2097152 | bytes 2113536 | tf_op jit(solution)/shard_map/kscui,kju->kscij/dot_general | solution.py:65
  35.0 16.1 %fusion.14.patch_ref = bf16[32,2,2,128,128]{4,3,2,1,0:T(8,128)(2,1)} fusion(s32[32,128]{1,0:T(8,128)S(1)} %get-tuple-element.15, bf16[2,2,512,512]{3,2,1,0:T(8,128)(2,1)S(1)} %copy-done, bf16[32]{0:T(256)(128)(2,1)S(1)} %slice_bitcast_fusion.1, pred[32,128,512,1,1]{2,1,4,3,0:T(32,128)(4,1)} %fusion.55), kind=kOutput, calls=%fused_computation.12 | convolution fusion | flops 10752098304 | bytes 8405056 | tf_op jit(solution)/shard_map/kscui,kju->kscij/dot_general | solution.py:65
  51.1 7.8 %all-to-all-done.1 = f32[8,4,128,128]{3,2,1,0:T(8,128)} async-done(((f32[8,4,128,128]{3,2,1,0:T(8,128)}), f32[8,4,128,128]{3,2,1,0:T(8,128)}, u32[]{:S(2)}, u32[]{:S(2)}) %all-to-all-start.1) | async-done | bytes 2097184 | tf_op jit(solution)/shard_map/all_to_all | solution.py:395
  58.9 74.6 %shard_map.77 = (f32[32,2,2,128,128]{4,3,2,1,0:T(8,128)}, f32[2,2,128,128]{3,2,1,0:T(8,128)}) custom-call(bf16[32,2,2,128,128]{4,3,2,1,0:T(8,128)(2,1)} %fusion.14.patch_ref, f32[32,128,128]{2,1,0:T(8,128)} %bitcast.17.measured_ref, f32[2,2,128,128]{3,2,1,0:T(8,128)} %bitcast.79, f32[2,128,128]{2,1,0:T(8,128)} %pad_maximum_fusion.6.kern_ref, ...), custom_call_target="tpu_custom_call" | custom-call | tf_op jit(solution)/shard_map/pallas_call | solution.py:341
  133.4 1.0 broadcast_multiply_fusion
  134.4 9.3 %all_to_all.25 = f32[8,1,8192]{2,1,0:T(1,128)S(1)} all-to-all(f32[8,1,8192]{2,1,0:T(1,128)S(1)} %bitcast.82), channel_id=1, replica_groups=mesh['group'=4,'member'=8] {'member'}, dimensions={0} | all-to-all | bytes 524288 | tf_op jit(solution)/shard_map/all_to_all | solution.py:367
  144.0 0.8 broadcast_in_dim.5
  144.8 3.4 %all-to-all-start.3 = ((f32[8,1,8192]{2,1,0:T(1,128)}), f32[8,1,8192]{2,1,0:T(1,128)S(1)}, u32[]{:S(2)}, u32[]{:S(2)}) async-start(f32[8,1,8192]{2,1,0:T(1,128)} %broadcast_in_dim.5), calls=%async_computation.3 | async-start | bytes 524288 | tf_op jit(solution)/shard_map/all_to_all | solution.py:370
  148.2 0.7 copy.19.requests
  148.9 13.8 %shard_map.78 = f32[2,2,512,512]{3,2,1,0:T(8,128)} custom-call(s32[32,3]{1,0:T(8,128)} %copy.19.requests, f32[1,1]{1,0:T(1,128)} %bitcast.2.peak_ref.peak, f32[32,2,2,128,128]{4,3,2,1,0:T(8,128)} %get-tuple-element.4.terms), custom_call_target="tpu_custom_call" | custom-call | tf_op jit(solution)/shard_map/pallas_call | solution.py:153
  162.7 0.7 copy.27
  (34 shorter events, 4.4 us)
Async XLA Ops:
  0.6 34.4 %copy-start = (bf16[2,2,512,512]{3,2,1,0:T(8,128)(2,1)S(1)}, bf16[2,2,512,512]{3,2,1,0:T(8,128)(2,1)}, u32[]{:S(2)}) copy-start(bf16[2,2,512,512]{3,2,1,0:T(8,128)(2,1)} %param.6) | copy-start | bytes 6291460
  0.6 13.3 %copy-start.3 = (s32[1,16,1]{1,2,0:T(1,128)S(1)}, s32[1,16,1]{1,2,0:T(1,128)}, u32[]{:S(2)}) copy-start(s32[1,16,1]{1,2,0:T(1,128)} %param.10) | copy-start | bytes 196
  0.7 13.3 %copy-start.2 = (f32[128,128]{1,0:T(8,128)S(1)}, f32[128,128]{1,0:T(8,128)}, u32[]{:S(2)}) copy-start(f32[128,128]{1,0:T(8,128)} %param.8) | copy-start | bytes 196612
  4.6 23.2 %all-to-all-start = ((s32[8,4,3]{1,2,0:T(4,128)}), s32[8,4,3]{1,2,0:T(4,128)S(1)}, u32[]{:S(2)}, u32[]{:S(2)}) async-start(s32[8,4,3]{1,2,0:T(4,128)} %copy.17), calls=%async_computation | async-start | bytes 32768 | tf_op jit(solution)/shard_map/all_to_all | solution.py:389
  11.4 9.9 %collective-permute-start = (f32[]{:T(128)}, f32[]{:T(128)}, u32[]{:S(2)}, u32[]{:S(2)}) collective-permute-start(f32[]{:T(128)} %reduce_max.9), channel_id=1, source_target_pairs={{0,8},{8,0},{16,24},{24,16},{1,9},{9,1},{17,25},{25,17},{2,10},{10... | collective-permute-start | bytes 20 | tf_op jit(solution)/shard_map/ppermute | solution.py:167
  15.2 3.2 %copy-start.1 = (f32[1,16,128,128]{3,2,1,0:T(8,128)S(1)}, f32[1,16,128,128]{3,2,1,0:T(8,128)}, u32[]{:S(2)}) copy-start(f32[1,16,128,128]{3,2,1,0:T(8,128)} %param.9) | copy-start | bytes 3145732
  22.6 4.6 %collective-permute-start.1 = (f32[]{:T(128)}, f32[]{:T(128)}, u32[]{:S(2)}, u32[]{:S(2)}) collective-permute-start(f32[]{:T(128)} %max.6), channel_id=1, source_target_pairs={{0,16},{8,24},{16,0},{24,8},{1,17},{9,25},{17,1},{25,9},{2,18},{10... | collective-permute-start | bytes 20 | tf_op jit(solution)/shard_map/ppermute | solution.py:167
  27.9 31.0 %all-to-all-start.1 = ((f32[8,4,128,128]{3,2,1,0:T(8,128)}), f32[8,4,128,128]{3,2,1,0:T(8,128)}, u32[]{:S(2)}, u32[]{:S(2)}) async-start(f32[8,4,128,128]{3,2,1,0:T(8,128)} %bitcast.78), calls=%async_computation.1 | async-start | bytes 4194304 | tf_op jit(solution)/shard_map/all_to_all | solution.py:395
  144.8 17.9 %all-to-all-start.3 = ((f32[8,1,8192]{2,1,0:T(1,128)}), f32[8,1,8192]{2,1,0:T(1,128)S(1)}, u32[]{:S(2)}, u32[]{:S(2)}) async-start(f32[8,1,8192]{2,1,0:T(1,128)} %broadcast_in_dim.5), calls=%async_computation.3 | async-start | bytes 524288 | tf_op jit(solution)/shard_map/all_to_all | solution.py:370

commit v10 on v9

--- a/solution.py
+++ b/solution.py
@@ -213,7 +213,7 @@
         probe_sum_ref[...] = jnp.zeros_like(probe_sum_ref)
 
     held = patch_ref.shape[0]
-    together = math.gcd(held, 4)
+    together = held
     for first in range(0, held, together):
         propagate_group(list(range(first, first + together)), patch_ref, measured_ref, probe_ref,
                         kern_ref, mats_right, mats_left, grad_ref, probe_sum_ref)

time: 164 us -> 159 us (0.970)
  Pallas kernels: 88.4 us -> 83.3 us
    pallas_call x1, Pallas kernels: 74.6 us -> 69.4 us  [propagate(): pl.pallas_call(propagate_kernel, grid=(count // held,), in_specs=[pl.Bloc...]
  transfers between devices with their start and end apart: 5 -> 5, of which waited for: 2 -> 2; matrix products, arithmetic and copies ran while one was open for 18% -> 19% of each run, Pallas kernels for 8% -> 9%
where the time goes in v10:
time: 159 us; the launch traced here: 158 us
  Pallas kernels  83.3 us (52%)
  starting transfers between devices  18.5 us (12%)
  matrix products  16.1 us (10%)
  other arithmetic  11.5 us (7%)
  blocking collectives  9.35 us (6%)
  local copies, waits for them, and re-layouts  8.49 us (5%)
  waiting for transfers between devices  8.37 us (5%)
  between operations  2.67 us (2%)
    pallas_call x1, Pallas kernels, propagate(): pl.pallas_call(propagate_kernel, grid=(count // held,), in_specs=[pl.Bloc...  69.4 us
    dot_general x1, matrix products, cut_windows(): jnp.einsum('kscui,kju->kscij', rows, col_sel, preferred_element_type=jnp....  16.1 us
    pallas_call x1, Pallas kernels, accumulate(): pl.pallas_call(place_kernel, grid_spec=grid_spec, out_shape=jax.ShapeDtyp...  13.9 us
    all_to_all x1, blocking collectives, member_sum(): lax.all_to_all(flat, 'member', split_axis=0, concat_axis=0, tiled=True)  9.35 us
    all_to_all x1, waiting for transfers between devices, on_device(): lax.all_to_all(sent.reshape(members, capacity, patch_side, patch_side), '...  7.75 us
    ppermute x2, starting transfers between devices, group_max(): value = jnp.maximum(value, lax.ppermute(value, 'group', pairs))  5.57 us
    all_to_all x1, starting transfers between devices, on_device(): lax.all_to_all(outgoing.reshape(members, capacity, 3), 'member', split_ax...  5.17 us
    all_to_all x1, starting transfers between devices, on_device(): lax.all_to_all(sent.reshape(members, capacity, patch_side, patch_side), '...  4.37 us
  transfers between devices with their start and end apart: 5, of which 2 were waited for; matrix products, arithmetic and copies ran while one was open for 19% of the time, Pallas kernels for 9%

profile of v10, /device:TPU:0, one launch (start us, length us, event | category | flops | bytes accessed | tf_op | source)
XLA Modules:
  0.0 158.4 jit_solution(18173460155118480882)
XLA Ops:
  0.7 0.9 fusion.38
  1.6 0.8 select_reduce_fusion
  2.4 0.7 multiply_add_fusion
  3.2 0.7 concatenate.33
  4.6 5.2 %all-to-all-start = ((s32[8,4,3]{1,2,0:T(4,128)}), s32[8,4,3]{1,2,0:T(4,128)S(1)}, u32[]{:S(2)}, u32[]{:S(2)}) async-start(s32[8,4,3]{1,2,0:T(4,128)} %copy.17), calls=%async_computation | async-start | bytes 32768 | tf_op jit(solution)/shard_map/all_to_all | solution.py:389
  9.8 1.0 multiply_reduce_fusion
  11.4 1.6 collective-permute-start
  14.2 1.0 pad_maximum_fusion.mats_right
  15.2 0.9 pad_maximum_fusion.1.mats_left
  16.8 1.6 %broadcast_in_dim.4 = f32[32,128,128]{2,1,0:T(8,128)} broadcast(f32[]{:T(128)} %constant.17.clone.1), dimensions={} | broadcast | bytes 2097156 | tf_op jit(solution)/shard_map/broadcast_in_dim | solution.py:392
  18.4 2.9 %scatter_fusion = f32[32,128,128]{2,1,0:T(8,128)} fusion(f32[32,128,128]{2,1,0:T(8,128)} %broadcast_in_dim.4, s32[16]{0:T(128)S(1)} %fusion.40, f32[16,128,128]{2,1,0:T(8,128)S(1)} %bitcast.80), kind=kCustom, calls=%fused_computation | custom fusion | bytes 3145792 | tf_op jit(solution)/shard_map/scatter | solution.py:392
  22.6 4.0 %collective-permute-start.1 = (f32[]{:T(128)}, f32[]{:T(128)}, u32[]{:S(2)}, u32[]{:S(2)}) collective-permute-start(f32[]{:T(128)} %max.6), channel_id=1, source_target_pairs={{0,16},{8,24},{16,0},{24,8},{1,17},{9,25},{17,1},{25,9},{2,18},{10... | collective-permute-start | bytes 20 | tf_op jit(solution)/shard_map/ppermute | solution.py:167
  27.8 4.4 %all-to-all-start.1 = ((f32[8,4,128,128]{3,2,1,0:T(8,128)}), f32[8,4,128,128]{3,2,1,0:T(8,128)}, u32[]{:S(2)}, u32[]{:S(2)}) async-start(f32[8,4,128,128]{3,2,1,0:T(8,128)} %bitcast.78), calls=%async_computation.1 | async-start | bytes 4194304 | tf_op jit(solution)/shard_map/all_to_all | solution.py:395
  32.4 2.6 %fusion.55 = pred[32,128,512,1,1]{2,1,4,3,0:T(32,128)(4,1)} fusion(s32[32,128]{1,0:T(8,128)S(1)} %get-tuple-element.14), kind=kLoop, calls=%fused_computation.8.clone.clone.clone.clone.2 | loop fusion | flops 2097152 | bytes 2113536 | tf_op jit(solution)/shard_map/kscui,kju->kscij/dot_general | solution.py:65
  35.0 16.1 %fusion.14.patch_ref = bf16[32,2,2,128,128]{4,3,2,1,0:T(8,128)(2,1)} fusion(s32[32,128]{1,0:T(8,128)S(1)} %get-tuple-element.15, bf16[2,2,512,512]{3,2,1,0:T(8,128)(2,1)S(1)} %copy-done, bf16[32]{0:T(256)(128)(2,1)S(1)} %slice_bitcast_fusion.1, pred[32,128,512,1,1]{2,1,4,3,0:T(32,128)(4,1)} %fusion.55), kind=kOutput, calls=%fused_computation.12 | convolution fusion | flops 10752098304 | bytes 8405056 | tf_op jit(solution)/shard_map/kscui,kju->kscij/dot_general | solution.py:65
  51.1 7.7 %all-to-all-done.1 = f32[8,4,128,128]{3,2,1,0:T(8,128)} async-done(((f32[8,4,128,128]{3,2,1,0:T(8,128)}), f32[8,4,128,128]{3,2,1,0:T(8,128)}, u32[]{:S(2)}, u32[]{:S(2)}) %all-to-all-start.1) | async-done | bytes 2097184 | tf_op jit(solution)/shard_map/all_to_all | solution.py:395
  58.9 69.4 %shard_map.77 = (f32[32,2,2,128,128]{4,3,2,1,0:T(8,128)}, f32[2,2,128,128]{3,2,1,0:T(8,128)}) custom-call(bf16[32,2,2,128,128]{4,3,2,1,0:T(8,128)(2,1)} %fusion.14.patch_ref, f32[32,128,128]{2,1,0:T(8,128)} %bitcast.17.measured_ref, f32[2,2,128,128]{3,2,1,0:T(8,128)} %bitcast.79, f32[2,128,128]{2,1,0:T(8,128)} %pad_maximum_fusion.6.kern_ref, ...), custom_call_target="tpu_custom_call" | custom-call | tf_op jit(solution)/shard_map/pallas_call | solution.py:341
  128.3 1.0 broadcast_multiply_fusion
  129.2 9.3 %all_to_all.25 = f32[8,1,8192]{2,1,0:T(1,128)S(1)} all-to-all(f32[8,1,8192]{2,1,0:T(1,128)S(1)} %bitcast.82), channel_id=1, replica_groups=mesh['group'=4,'member'=8] {'member'}, dimensions={0} | all-to-all | bytes 524288 | tf_op jit(solution)/shard_map/all_to_all | solution.py:367
  138.8 0.8 broadcast_in_dim.5
  139.6 3.4 %all-to-all-start.3 = ((f32[8,1,8192]{2,1,0:T(1,128)}), f32[8,1,8192]{2,1,0:T(1,128)S(1)}, u32[]{:S(2)}, u32[]{:S(2)}) async-start(f32[8,1,8192]{2,1,0:T(1,128)} %broadcast_in_dim.5), calls=%async_computation.3 | async-start | bytes 524288 | tf_op jit(solution)/shard_map/all_to_all | solution.py:370
  143.0 0.7 copy.19.requests
  143.7 13.9 %shard_map.78 = f32[2,2,512,512]{3,2,1,0:T(8,128)} custom-call(s32[32,3]{1,0:T(8,128)} %copy.19.requests, f32[1,1]{1,0:T(1,128)} %bitcast.2.peak_ref.peak, f32[32,2,2,128,128]{4,3,2,1,0:T(8,128)} %get-tuple-element.4.terms), custom_call_target="tpu_custom_call" | custom-call | tf_op jit(solution)/shard_map/pallas_call | solution.py:153
  157.7 0.7 copy.27
  (34 shorter events, 4.4 us)
Async XLA Ops:
  0.6 34.4 %copy-start = (bf16[2,2,512,512]{3,2,1,0:T(8,128)(2,1)S(1)}, bf16[2,2,512,512]{3,2,1,0:T(8,128)(2,1)}, u32[]{:S(2)}) copy-start(bf16[2,2,512,512]{3,2,1,0:T(8,128)(2,1)} %param.6) | copy-start | bytes 6291460
  0.6 13.3 %copy-start.3 = (s32[1,16,1]{1,2,0:T(1,128)S(1)}, s32[1,16,1]{1,2,0:T(1,128)}, u32[]{:S(2)}) copy-start(s32[1,16,1]{1,2,0:T(1,128)} %param.10) | copy-start | bytes 196
  0.7 13.3 %copy-start.2 = (f32[128,128]{1,0:T(8,128)S(1)}, f32[128,128]{1,0:T(8,128)}, u32[]{:S(2)}) copy-start(f32[128,128]{1,0:T(8,128)} %param.8) | copy-start | bytes 196612
  4.6 23.2 %all-to-all-start = ((s32[8,4,3]{1,2,0:T(4,128)}), s32[8,4,3]{1,2,0:T(4,128)S(1)}, u32[]{:S(2)}, u32[]{:S(2)}) async-start(s32[8,4,3]{1,2,0:T(4,128)} %copy.17), calls=%async_computation | async-start | bytes 32768 | tf_op jit(solution)/shard_map/all_to_all | solution.py:389
  11.4 9.9 %collective-permute-start = (f32[]{:T(128)}, f32[]{:T(128)}, u32[]{:S(2)}, u32[]{:S(2)}) collective-permute-start(f32[]{:T(128)} %reduce_max.9), channel_id=1, source_target_pairs={{0,8},{8,0},{16,24},{24,16},{1,9},{9,1},{17,25},{25,17},{2,10},{10... | collective-permute-start | bytes 20 | tf_op jit(solution)/shard_map/ppermute | solution.py:167
  15.2 3.2 %copy-start.1 = (f32[1,16,128,128]{3,2,1,0:T(8,128)S(1)}, f32[1,16,128,128]{3,2,1,0:T(8,128)}, u32[]{:S(2)}) copy-start(f32[1,16,128,128]{3,2,1,0:T(8,128)} %param.9) | copy-start | bytes 3145732
  22.6 4.6 %collective-permute-start.1 = (f32[]{:T(128)}, f32[]{:T(128)}, u32[]{:S(2)}, u32[]{:S(2)}) collective-permute-start(f32[]{:T(128)} %max.6), channel_id=1, source_target_pairs={{0,16},{8,24},{16,0},{24,8},{1,17},{9,25},{17,1},{25,9},{2,18},{10... | collective-permute-start | bytes 20 | tf_op jit(solution)/shard_map/ppermute | solution.py:167
  27.8 31.0 %all-to-all-start.1 = ((f32[8,4,128,128]{3,2,1,0:T(8,128)}), f32[8,4,128,128]{3,2,1,0:T(8,128)}, u32[]{:S(2)}, u32[]{:S(2)}) async-start(f32[8,4,128,128]{3,2,1,0:T(8,128)} %bitcast.78), calls=%async_computation.1 | async-start | bytes 4194304 | tf_op jit(solution)/shard_map/all_to_all | solution.py:395
  139.6 18.0 %all-to-all-start.3 = ((f32[8,1,8192]{2,1,0:T(1,128)}), f32[8,1,8192]{2,1,0:T(1,128)S(1)}, u32[]{:S(2)}, u32[]{:S(2)}) async-start(f32[8,1,8192]{2,1,0:T(1,128)} %broadcast_in_dim.5), calls=%async_computation.3 | async-start | bytes 524288 | tf_op jit(solution)/shard_map/all_to_all | solution.py:370

commit v11 on v10

--- a/solution.py
+++ b/solution.py
@@ -131,7 +131,7 @@
 def accumulate(terms, requests, peak, tile_cells):
     slot_count, slice_count = terms.shape[:2]
     patch_side = terms.shape[-1]
-    held = math.gcd(slot_count, 8)
+    held = math.gcd(slot_count, 16)
     grid_spec = pltpu.PrefetchScalarGridSpec(
         num_scalar_prefetch=1,
         grid=(slot_count // held,),

time: 159 us -> 159 us (level)
  no operation moved by 1% of the time
where the time goes in v11:
time: 159 us; the launch traced here: 158 us
  Pallas kernels  83.4 us (52%)
  starting transfers between devices  18.5 us (12%)
  matrix products  16.1 us (10%)
  other arithmetic  11.5 us (7%)
  blocking collectives  9.35 us (6%)
  local copies, waits for them, and re-layouts  8.52 us (5%)
  waiting for transfers between devices  8.42 us (5%)
  between operations  2.67 us (2%)
    pallas_call x1, Pallas kernels, propagate(): pl.pallas_call(propagate_kernel, grid=(count // held,), in_specs=[pl.Bloc...  69.4 us
    dot_general x1, matrix products, cut_windows(): jnp.einsum('kscui,kju->kscij', rows, col_sel, preferred_element_type=jnp....  16.1 us
    pallas_call x1, Pallas kernels, accumulate(): pl.pallas_call(place_kernel, grid_spec=grid_spec, out_shape=jax.ShapeDtyp...  14 us
    all_to_all x1, blocking collectives, member_sum(): lax.all_to_all(flat, 'member', split_axis=0, concat_axis=0, tiled=True)  9.35 us
    all_to_all x1, waiting for transfers between devices, on_device(): lax.all_to_all(sent.reshape(members, capacity, patch_side, patch_side), '...  7.75 us
    ppermute x2, starting transfers between devices, group_max(): value = jnp.maximum(value, lax.ppermute(value, 'group', pairs))  5.52 us
    all_to_all x1, starting transfers between devices, on_device(): lax.all_to_all(outgoing.reshape(members, capacity, 3), 'member', split_ax...  5.17 us
    all_to_all x1, starting transfers between devices, on_device(): lax.all_to_all(sent.reshape(members, capacity, patch_side, patch_side), '...  4.37 us
  transfers between devices with their start and end apart: 5, of which 2 were waited for; matrix products, arithmetic and copies ran while one was open for 19% of the time, Pallas kernels for 9%

profile of v11, /device:TPU:0, one launch (start us, length us, event | category | flops | bytes accessed | tf_op | source)
XLA Modules:
  0.0 158.4 jit_solution(17141117825207611969)
XLA Ops:
  0.7 0.9 fusion.38
  1.6 0.8 select_reduce_fusion
  3.2 0.7 concatenate.33
  4.6 5.2 %all-to-all-start = ((s32[8,4,3]{1,2,0:T(4,128)}), s32[8,4,3]{1,2,0:T(4,128)S(1)}, u32[]{:S(2)}, u32[]{:S(2)}) async-start(s32[8,4,3]{1,2,0:T(4,128)} %copy.17), calls=%async_computation | async-start | bytes 32768 | tf_op jit(solution)/shard_map/all_to_all | solution.py:389
  9.8 1.0 multiply_reduce_fusion
  11.4 1.6 collective-permute-start
  14.2 1.0 pad_maximum_fusion.mats_right
  15.2 0.9 pad_maximum_fusion.1.mats_left
  16.8 1.6 %broadcast_in_dim.4 = f32[32,128,128]{2,1,0:T(8,128)} broadcast(f32[]{:T(128)} %constant.17.clone.1), dimensions={} | broadcast | bytes 2097156 | tf_op jit(solution)/shard_map/broadcast_in_dim | solution.py:392
  18.4 3.0 %scatter_fusion = f32[32,128,128]{2,1,0:T(8,128)} fusion(f32[32,128,128]{2,1,0:T(8,128)} %broadcast_in_dim.4, s32[16]{0:T(128)S(1)} %fusion.40, f32[16,128,128]{2,1,0:T(8,128)S(1)} %bitcast.80), kind=kCustom, calls=%fused_computation | custom fusion | bytes 3145792 | tf_op jit(solution)/shard_map/scatter | solution.py:392
  22.6 3.9 %collective-permute-start.1 = (f32[]{:T(128)}, f32[]{:T(128)}, u32[]{:S(2)}, u32[]{:S(2)}) collective-permute-start(f32[]{:T(128)} %max.6), channel_id=1, source_target_pairs={{0,16},{8,24},{16,0},{24,8},{1,17},{9,25},{17,1},{25,9},{2,18},{10... | collective-permute-start | bytes 20 | tf_op jit(solution)/shard_map/ppermute | solution.py:167
  26.6 0.7 collective-permute-done.1
  27.8 4.4 %all-to-all-start.1 = ((f32[8,4,128,128]{3,2,1,0:T(8,128)}), f32[8,4,128,128]{3,2,1,0:T(8,128)}, u32[]{:S(2)}, u32[]{:S(2)}) async-start(f32[8,4,128,128]{3,2,1,0:T(8,128)} %bitcast.78), calls=%async_computation.1 | async-start | bytes 4194304 | tf_op jit(solution)/shard_map/all_to_all | solution.py:395
  32.4 2.6 %fusion.55 = pred[32,128,512,1,1]{2,1,4,3,0:T(32,128)(4,1)} fusion(s32[32,128]{1,0:T(8,128)S(1)} %get-tuple-element.14), kind=kLoop, calls=%fused_computation.8.clone.clone.clone.clone.2 | loop fusion | flops 2097152 | bytes 2113536 | tf_op jit(solution)/shard_map/kscui,kju->kscij/dot_general | solution.py:65
  35.0 16.1 %fusion.14.patch_ref = bf16[32,2,2,128,128]{4,3,2,1,0:T(8,128)(2,1)} fusion(s32[32,128]{1,0:T(8,128)S(1)} %get-tuple-element.15, bf16[2,2,512,512]{3,2,1,0:T(8,128)(2,1)S(1)} %copy-done, bf16[32]{0:T(256)(128)(2,1)S(1)} %slice_bitcast_fusion.1, pred[32,128,512,1,1]{2,1,4,3,0:T(32,128)(4,1)} %fusion.55), kind=kOutput, calls=%fused_computation.12 | convolution fusion | flops 10752098304 | bytes 8405056 | tf_op jit(solution)/shard_map/kscui,kju->kscij/dot_general | solution.py:65
  51.1 7.7 %all-to-all-done.1 = f32[8,4,128,128]{3,2,1,0:T(8,128)} async-done(((f32[8,4,128,128]{3,2,1,0:T(8,128)}), f32[8,4,128,128]{3,2,1,0:T(8,128)}, u32[]{:S(2)}, u32[]{:S(2)}) %all-to-all-start.1) | async-done | bytes 2097184 | tf_op jit(solution)/shard_map/all_to_all | solution.py:395
  58.9 69.4 %shard_map.77 = (f32[32,2,2,128,128]{4,3,2,1,0:T(8,128)}, f32[2,2,128,128]{3,2,1,0:T(8,128)}) custom-call(bf16[32,2,2,128,128]{4,3,2,1,0:T(8,128)(2,1)} %fusion.14.patch_ref, f32[32,128,128]{2,1,0:T(8,128)} %bitcast.17.measured_ref, f32[2,2,128,128]{3,2,1,0:T(8,128)} %bitcast.79, f32[2,128,128]{2,1,0:T(8,128)} %pad_maximum_fusion.6.kern_ref, ...), custom_call_target="tpu_custom_call" | custom-call | tf_op jit(solution)/shard_map/pallas_call | solution.py:341
  128.3 1.0 broadcast_multiply_fusion
  129.3 9.3 %all_to_all.25 = f32[8,1,8192]{2,1,0:T(1,128)S(1)} all-to-all(f32[8,1,8192]{2,1,0:T(1,128)S(1)} %bitcast.82), channel_id=1, replica_groups=mesh['group'=4,'member'=8] {'member'}, dimensions={0} | all-to-all | bytes 524288 | tf_op jit(solution)/shard_map/all_to_all | solution.py:367
  138.8 0.8 broadcast_in_dim.5
  139.7 3.4 %all-to-all-start.3 = ((f32[8,1,8192]{2,1,0:T(1,128)}), f32[8,1,8192]{2,1,0:T(1,128)S(1)}, u32[]{:S(2)}, u32[]{:S(2)}) async-start(f32[8,1,8192]{2,1,0:T(1,128)} %broadcast_in_dim.5), calls=%async_computation.3 | async-start | bytes 524288 | tf_op jit(solution)/shard_map/all_to_all | solution.py:370
  143.1 0.7 copy.19.requests
  143.8 14.0 %shard_map.78 = f32[2,2,512,512]{3,2,1,0:T(8,128)} custom-call(s32[32,3]{1,0:T(8,128)} %copy.19.requests, f32[1,1]{1,0:T(1,128)} %bitcast.2.peak_ref.peak, f32[32,2,2,128,128]{4,3,2,1,0:T(8,128)} %get-tuple-element.4.terms), custom_call_target="tpu_custom_call" | custom-call | tf_op jit(solution)/shard_map/pallas_call | solution.py:153
  157.7 0.7 copy.27
  (34 shorter events, 4.4 us)
Async XLA Ops:
  0.6 34.4 %copy-start = (bf16[2,2,512,512]{3,2,1,0:T(8,128)(2,1)S(1)}, bf16[2,2,512,512]{3,2,1,0:T(8,128)(2,1)}, u32[]{:S(2)}) copy-start(bf16[2,2,512,512]{3,2,1,0:T(8,128)(2,1)} %param.6) | copy-start | bytes 6291460
  0.6 13.3 %copy-start.3 = (s32[1,16,1]{1,2,0:T(1,128)S(1)}, s32[1,16,1]{1,2,0:T(1,128)}, u32[]{:S(2)}) copy-start(s32[1,16,1]{1,2,0:T(1,128)} %param.10) | copy-start | bytes 196
  0.7 13.3 %copy-start.2 = (f32[128,128]{1,0:T(8,128)S(1)}, f32[128,128]{1,0:T(8,128)}, u32[]{:S(2)}) copy-start(f32[128,128]{1,0:T(8,128)} %param.8) | copy-start | bytes 196612
  4.6 23.2 %all-to-all-start = ((s32[8,4,3]{1,2,0:T(4,128)}), s32[8,4,3]{1,2,0:T(4,128)S(1)}, u32[]{:S(2)}, u32[]{:S(2)}) async-start(s32[8,4,3]{1,2,0:T(4,128)} %copy.17), calls=%async_computation | async-start | bytes 32768 | tf_op jit(solution)/shard_map/all_to_all | solution.py:389
  11.4 9.9 %collective-permute-start = (f32[]{:T(128)}, f32[]{:T(128)}, u32[]{:S(2)}, u32[]{:S(2)}) collective-permute-start(f32[]{:T(128)} %reduce_max.9), channel_id=1, source_target_pairs={{0,8},{8,0},{16,24},{24,16},{1,9},{9,1},{17,25},{25,17},{2,10},{10... | collective-permute-start | bytes 20 | tf_op jit(solution)/shard_map/ppermute | solution.py:167
  15.2 3.2 %copy-start.1 = (f32[1,16,128,128]{3,2,1,0:T(8,128)S(1)}, f32[1,16,128,128]{3,2,1,0:T(8,128)}, u32[]{:S(2)}) copy-start(f32[1,16,128,128]{3,2,1,0:T(8,128)} %param.9) | copy-start | bytes 3145732
  22.6 4.6 %collective-permute-start.1 = (f32[]{:T(128)}, f32[]{:T(128)}, u32[]{:S(2)}, u32[]{:S(2)}) collective-permute-start(f32[]{:T(128)} %max.6), channel_id=1, source_target_pairs={{0,16},{8,24},{16,0},{24,8},{1,17},{9,25},{17,1},{25,9},{2,18},{10... | collective-permute-start | bytes 20 | tf_op jit(solution)/shard_map/ppermute | solution.py:167
  27.8 31.0 %all-to-all-start.1 = ((f32[8,4,128,128]{3,2,1,0:T(8,128)}), f32[8,4,128,128]{3,2,1,0:T(8,128)}, u32[]{:S(2)}, u32[]{:S(2)}) async-start(f32[8,4,128,128]{3,2,1,0:T(8,128)} %bitcast.78), calls=%async_computation.1 | async-start | bytes 4194304 | tf_op jit(solution)/shard_map/all_to_all | solution.py:395
  139.7 18.1 %all-to-all-start.3 = ((f32[8,1,8192]{2,1,0:T(1,128)}), f32[8,1,8192]{2,1,0:T(1,128)S(1)}, u32[]{:S(2)}, u32[]{:S(2)}) async-start(f32[8,1,8192]{2,1,0:T(1,128)} %broadcast_in_dim.5), calls=%async_computation.3 | async-start | bytes 524288 | tf_op jit(solution)/shard_map/all_to_all | solution.py:370
